TPU v7x, 128 devices: a whole 4x4x4 slice. The times are simulated.
128 devices in a mesh: ctx: 8 (over z, x_hi), head: 16 (over x_lo, y, core).
Axes of the slice: x: 4 (x_hi: 2, x_lo: 2; x = x_hi * 2 + x_lo), y: 4, z: 4, core: 2. Of those that a mesh axis runs over, the one named last changes fastest.
Arguments:
- queries: bfloat16 [32768, 4096], P(('ctx', 'head')), may hold values from -8 to 8
- keys: bfloat16 [32768, 2048], P(('ctx', 'head')), may hold values from -8 to 8
- values: bfloat16 [32768, 2048], P(('ctx', 'head')), may hold values from -18 to 18
- grad_out: bfloat16 [32768, 4096], P(('ctx', 'head')), may hold values from -18 to 18
Outputs:
- attended: bfloat16 [32768, 4096], P(('ctx', 'head'))
- grad_queries: bfloat16 [32768, 4096], P(('ctx', 'head'))
- grad_keys: bfloat16 [32768, 2048], P(('ctx', 'head'))
- grad_values: bfloat16 [32768, 2048], P(('ctx', 'head'))
All inputs are finite; a program needn't handle non-finite values.
Results may differ from a plain program's by a relative error of at most 0.02.
Values may be sent and summed in bfloat16 or wider, within the bound.
No kernel may reach another device: no remote copies, remote signals or barrier semaphores. Data moves between devices by JAX's collectives and lax.ppermute only.
A program may use at most 256 MiB of HBM per device.

v0:
```python
import functools

import jax
import jax.numpy as jnp
from jax import lax
from jax.experimental import pallas as pl
from jax.experimental.pallas import tpu as pltpu
from jax.sharding import PartitionSpec as P

HD = 128
QH = 32
KVH = 16
WIN = 1024
QPRE = 168
BLK = 256


def shifted(block, axis, distance):
    devices = range(lax.axis_size(axis))
    route = [(i - distance, i) for i in devices if i - distance in devices]
    return lax.ppermute(block, axis, route)


def attend_kernel(first_ref, *refs, heads, block_offset, early, carry_od, acc_base):
    pos = 0
    q_refs, g_refs = [], []
    for _ in range(heads):
        q_refs.append(refs[pos])
        g_refs.append(refs[pos + 1])
        pos += 2
    if early:
        kt_ref, vt_ref, kg_ref, vg_ref = refs[pos : pos + 4]
        pos += 4
    else:
        k_ref, v_ref = refs[pos : pos + 2]
        pos += 2
    pos += sum(carry_od)
    od_refs = refs[pos : pos + heads]
    pos += heads
    dk_ref, dv_ref, bias_ref = refs[pos : pos + 3]
    pos += 3
    if early:
        kx_ref, vx_ref = refs[pos : pos + 2]
    step = pl.program_id(0)
    block = step + block_offset
    rows = q_refs[0].shape[0]
    span = WIN + rows
    scale = QPRE ** (-0.5)

    @pl.when(step == 0)
    def _():
        dk_ref[...] = jnp.zeros_like(dk_ref)
        dv_ref[...] = jnp.zeros_like(dv_ref)
        row_id = lax.broadcasted_iota(jnp.int32, (rows, span), 0)
        col_id = lax.broadcasted_iota(jnp.int32, (rows, span), 1)
        distance = row_id + WIN - col_id
        band = (distance >= 0) & (distance < WIN)
        bias_ref[...] = jnp.where(band, 0.0, -jnp.inf).astype(jnp.float32)
        if early:
            kx_ref[:WIN, :] = kt_ref[...]
            kx_ref[WIN:, :] = kg_ref[...]
            vx_ref[:WIN, :] = vt_ref[...]
            vx_ref[WIN:, :] = vg_ref[...]

    start = pl.multiple_of(block * rows, rows)
    if early:
        k_win = kx_ref[pl.ds(start, span), :]
        v_win = vx_ref[pl.ds(start, span), :]
        col_id = lax.broadcasted_iota(jnp.int32, (rows, span), 1)
        key_pos = first_ref[0] - WIN + start + col_id
        bias = jnp.where(key_pos >= 0, bias_ref[...], -jnp.inf)
    else:
        key_start = pl.multiple_of(start - WIN, rows)
        k_win = k_ref[pl.ds(key_start, span), :]
        v_win = v_ref[pl.ds(key_start, span), :]
        bias = bias_ref[...]
    nt = (((1,), (1,)), ((), ()))
    tn = (((0,), (0,)), ((), ()))
    dk_acc = None
    dv_acc = None
    for q_ref, g_ref, od_ref in zip(q_refs, g_refs, od_refs):
        q = q_ref[...]
        g = g_ref[...]
        scores = lax.dot_general(q, k_win, nt, preferred_element_type=jnp.float32) * scale
        scores = scores + bias
        largest = jnp.max(scores, axis=-1, keepdims=True)
        unnormed = jnp.exp(scores - largest)
        probs = unnormed * (1.0 / jnp.sum(unnormed, axis=-1, keepdims=True))
        probs_low = probs.astype(jnp.bfloat16)
        out = jnp.dot(probs_low, v_win, preferred_element_type=jnp.float32).astype(jnp.bfloat16)
        od_ref[:, :HD] = out
        grad_probs = lax.dot_general(g, v_win, nt, preferred_element_type=jnp.float32)
        inner = jnp.sum(g.astype(jnp.float32) * out.astype(jnp.float32), axis=-1, keepdims=True)
        grad_scores = (probs * (grad_probs - inner) * scale).astype(jnp.bfloat16)
        od_ref[:, HD:] = jnp.dot(grad_scores, k_win, preferred_element_type=jnp.float32).astype(
            jnp.bfloat16
        )
        dk_part = lax.dot_general(grad_scores, q, tn, preferred_element_type=jnp.float32)
        dv_part = lax.dot_general(probs_low, g, tn, preferred_element_type=jnp.float32)
        dk_acc = dk_part if dk_acc is None else dk_acc + dk_part
        dv_acc = dv_part if dv_acc is None else dv_acc + dv_part
    acc_start = pl.multiple_of(start - acc_base, rows)
    dk_ref[pl.ds(acc_start, span), :] += dk_acc
    dv_ref[pl.ds(acc_start, span), :] += dv_acc


def attend(sources, first_part, tail, first_query, blocks, carried_od):
    heads = len(sources)
    query_count = first_part.shape[0]
    acc_base = 0 if tail is not None else WIN
    acc_rows = 2 * WIN if tail is not None else query_count
    rows = BLK
    span = WIN + rows
    block_offset, block_count = blocks
    early = tail is not None
    first = jnp.reshape(first_query, (1,)).astype(jnp.int32)
    whole = pl.BlockSpec((acc_rows, HD), lambda b, f: (0, 0))
    in_specs = []
    operands = [first]
    for source, q_col, g_col in sources:
        in_specs += [
            pl.BlockSpec((rows, HD), lambda b, f, c=q_col: (b + block_offset, c)),
            pl.BlockSpec((rows, HD), lambda b, f, c=g_col: (b + block_offset, c)),
        ]
        operands += [source, source]
    if early:
        piece = (WIN, HD)
        in_specs += [
            pl.BlockSpec(piece, lambda b, f: (0, 0)),
            pl.BlockSpec(piece, lambda b, f: (0, 1)),
            pl.BlockSpec(piece, lambda b, f: (0, 0)),
            pl.BlockSpec(piece, lambda b, f: (0, 1)),
        ]
        operands += [tail, tail, first_part, first_part]
    else:
        in_specs += [
            pl.BlockSpec((query_count, HD), lambda b, f: (0, 0)),
            pl.BlockSpec((query_count, HD), lambda b, f: (0, 1)),
        ]
        operands += [first_part, first_part]
    aliases = {}
    carry_od = tuple(od is not None for od in carried_od)
    for i, od in enumerate(carried_od):
        if od is not None:
            aliases[len(operands)] = i
            in_specs.append(pl.BlockSpec(memory_space=pl.ANY))
            operands.append(od)
    scratch = [pltpu.VMEM((rows, span), jnp.float32)]
    if early:
        scratch += [pltpu.VMEM((2 * WIN, HD), jnp.bfloat16)] * 2
    grid_spec = pltpu.PrefetchScalarGridSpec(
        num_scalar_prefetch=1,
        grid=(block_count,),
        in_specs=in_specs,
        out_specs=[pl.BlockSpec((rows, 2 * HD), lambda b, f: (b + block_offset, 0))] * heads
        + [whole, whole],
        scratch_shapes=scratch,
    )
    kernel = functools.partial(
        attend_kernel,
        heads=heads,
        block_offset=block_offset,
        early=early,
        carry_od=carry_od,
        acc_base=acc_base,
    )
    return pl.pallas_call(
        kernel,
        grid_spec=grid_spec,
        out_shape=[jax.ShapeDtypeStruct((query_count, 2 * HD), jnp.bfloat16)] * heads
        + [
            jax.ShapeDtypeStruct((acc_rows, HD), jnp.float32),
            jax.ShapeDtypeStruct((acc_rows, HD), jnp.float32),
        ],
        input_output_aliases=aliases,
        compiler_params=pltpu.CompilerParams(
            dimension_semantics=("arbitrary",), vmem_limit_bytes=56 * 1024 * 1024
        ),
    )(*operands)


def exchange_in(pieces):
    stacked = jnp.transpose(jnp.concatenate(pieces, axis=-1), (1, 0, 2))
    moved = lax.all_to_all(stacked, "head", split_axis=0, concat_axis=0, tiled=True)
    return moved.reshape(moved.shape[0] * moved.shape[1], moved.shape[2])


def exchange_out(group_block):
    shared = lax.axis_size("head")
    split = group_block.reshape(shared, group_block.shape[0] // shared, group_block.shape[1])
    moved = lax.all_to_all(split, "head", split_axis=0, concat_axis=0, tiled=True)
    return jnp.transpose(moved, (1, 0, 2))


def body(queries, keys, values, grad_out):
    token_count = queries.shape[0]
    shared = KVH
    pair = (QH // KVH) * HD
    query_rows = queries.reshape(token_count, shared, pair)
    grad_rows = grad_out.reshape(token_count, shared, pair)
    key_rows = keys.reshape(token_count, shared, HD)
    value_rows = values.reshape(token_count, shared, HD)
    first_part = exchange_in(
        [key_rows, value_rows, query_rows[:, :, :HD], grad_rows[:, :, :HD]]
    )
    second_part = exchange_in([query_rows[:, :, HD:], grad_rows[:, :, HD:]])
    group_rows = first_part.shape[0]
    block_total = group_rows // BLK
    lead = WIN // BLK
    first_query = lax.axis_index("ctx") * group_rows
    tail = shifted(first_part[group_rows - WIN :, : 2 * HD], "ctx", 1)
    late = (lead, block_total - lead)
    early = (0, lead)
    head0 = (first_part, 2, 3)
    head1 = (second_part, 0, 1)
    first_out, key_late, value_late = attend([head0], first_part, None, first_query, late, (None,))
    first_out, second_out, key_early, value_early = attend(
        [head0, head1], first_part, tail, first_query, early, (first_out, None)
    )
    back = shifted(
        jnp.concatenate([key_early[:WIN], value_early[:WIN]], axis=1).astype(jnp.bfloat16),
        "ctx",
        -1,
    ).astype(jnp.float32)
    second_out, key_last, value_last = attend(
        [head1], first_part, None, first_query, late, (second_out,)
    )
    first_back = exchange_out(first_out)
    second_back = exchange_out(second_out)
    lead_pad = ((0, group_rows - WIN), (0, 0))
    tail_pad = ((group_rows - WIN, 0), (0, 0))
    key_grad = (
        key_late + key_last + jnp.pad(key_early[WIN:], lead_pad) + jnp.pad(back[:, :HD], tail_pad)
    ).astype(jnp.bfloat16)
    value_grad = (
        value_late
        + value_last
        + jnp.pad(value_early[WIN:], lead_pad)
        + jnp.pad(back[:, HD:], tail_pad)
    ).astype(jnp.bfloat16)
    grads_back = exchange_out(jnp.concatenate([key_grad, value_grad], axis=1))
    attended = jnp.concatenate([first_back[:, :, :HD], second_back[:, :, :HD]], axis=2)
    grad_queries = jnp.concatenate([first_back[:, :, HD:], second_back[:, :, HD:]], axis=2)
    return (
        attended.reshape(token_count, QH * HD),
        grad_queries.reshape(token_count, QH * HD),
        grads_back[:, :, :HD].reshape(token_count, KVH * HD),
        grads_back[:, :, HD:].reshape(token_count, KVH * HD),
    )


def solution(mesh):
    placed = (
        P(("ctx", "head"), None),
        P(("ctx", "head"), None),
        P(("ctx", "head"), None),
        P(("ctx", "head"), None),
    )
    return jax.shard_map(
        body,
        mesh=mesh,
        in_specs=placed,
        out_specs=(
            P(("ctx", "head"), None),
            P(("ctx", "head"), None),
            P(("ctx", "head"), None),
            P(("ctx", "head"), None),
        ),
        check_vma=False,
    )
```

profile of v0, /device:TPU:121, one launch (start us, length us, event | category | flops | bytes accessed | tf_op | source)
XLA Modules:
  0.0 281.8 jit_solution(16044622326982191236)
XLA Ops:
  0.6 2.3 copy.30
  3.6 1.3 copy-done.6
  6.3 0.9 copy-done.9
  7.7 2.3 maximum_bitcast_fusion
  10.1 5.9 %all-to-all-start = ((bf16[16,256,512]{2,1,0:T(8,128)(2,1)}), bf16[16,256,512]{2,1,0:T(8,128)(2,1)}, u32[]{:S(2)}, u32[]{:S(2)}) async-start(bf16[16,256,512]{2,1,0:T(8,128)(2,1)} %maximum_bitcast_fusion), calls=%async_computation | async-start | bytes 8388608 | tf_op jit(solution)/shard_map/all_to_all | solution.py:184
  16.5 1.6 maximum_bitcast_fusion.1
  18.1 59.2 %all-to-all-done = bf16[16,256,512]{2,1,0:T(8,128)(2,1)} async-done(((bf16[16,256,512]{2,1,0:T(8,128)(2,1)}), bf16[16,256,512]{2,1,0:T(8,128)(2,1)}, u32[]{:S(2)}, u32[]{:S(2)}) %all-to-all-start) | async-done | bytes 4194336 | tf_op jit(solution)/shard_map/all_to_all | solution.py:184
  77.3 5.9 %all-to-all-start.1 = ((bf16[16,256,256]{2,1,0:T(8,128)(2,1)}), bf16[16,256,256]{2,1,0:T(8,128)(2,1)S(1)}, u32[]{:S(2)}, u32[]{:S(2)}) async-start(bf16[16,256,256]{2,1,0:T(8,128)(2,1)} %maximum_bitcast_fusion.1), calls=%async_computation.1 | async-start | bytes 4194304 | tf_op jit(solution)/shard_map/all_to_all | solution.py:184
  83.3 1.1 slice.74
  84.3 4.5 %collective-permute-start = (bf16[1024,256]{1,0:T(8,128)(2,1)S(1)}, bf16[1024,256]{1,0:T(8,128)(2,1)S(1)}, u32[]{:S(2)}, u32[]{:S(2)}) collective-permute-start(bf16[1024,256]{1,0:T(8,128)(2,1)S(1)} %slice.74), channel_id=1, source_target_pairs={{0,16},{16,32},{32,48},{48,64},{64,80},{80,96},{96,112},{1,17},{17... | collective-permute-start | bytes 1572872 | tf_op jit(solution)/shard_map/ppermute | solution.py:21
  88.9 25.0 %shard_map.75 = (bf16[4096,256]{1,0:T(8,128)(2,1)}, f32[4096,128]{1,0:T(8,128)}, f32[4096,128]{1,0:T(8,128)}) custom-call(s32[1]{0:T(128)} %bitcast.first_ref, bf16[4096,512]{1,0:T(8,128)(2,1)} %bitcast.2.refs_0_.refs_1_.refs_2_.refs_3_.refs_6_.refs_7_, bf16[4096,512]{1,0:T(8,128)(2,1)} %bitcast.2.refs_0_.refs_1_.refs_2_.refs_3_.refs_6_.refs_7_, ...), custom_call_target="tpu_custom_call" | custom-call | tf_op jit(solution)/shard_map/pallas_call | solution.py:167
  113.9 6.8 %collective-permute-done.refs_4_.refs_5_ = bf16[1024,256]{1,0:T(8,128)(2,1)S(1)} collective-permute-done((bf16[1024,256]{1,0:T(8,128)(2,1)S(1)}, bf16[1024,256]{1,0:T(8,128)(2,1)S(1)}, u32[]{:S(2)}, u32[]{:S(2)}) %collective-permute-start) | collective-permute-done | bytes 524320 | tf_op jit(solution)/shard_map/ppermute | solution.py:21
  121.5 16.0 %shard_map.76 = (bf16[4096,256]{1,0:T(8,128)(2,1)}, bf16[4096,256]{1,0:T(8,128)(2,1)}, f32[2048,128]{1,0:T(8,128)}, f32[2048,128]{1,0:T(8,128)}) custom-call(s32[1]{0:T(128)} %bitcast.first_ref, bf16[4096,512]{1,0:T(8,128)(2,1)} %bitcast.2.refs_0_.refs_1_.refs_2_.refs_3_.refs_6_.refs_7_, ...), custom_call_target="tpu_custom_call", output_to_operand_aliasing={{0}: (9, {})} | custom-call | tf_op jit(solution)/shard_map/pallas_call | solution.py:167
  137.6 24.9 %shard_map.77 = (bf16[4096,256]{1,0:T(8,128)(2,1)}, f32[4096,128]{1,0:T(8,128)}, f32[4096,128]{1,0:T(8,128)}) custom-call(s32[1]{0:T(128)} %bitcast.first_ref, bf16[4096,256]{1,0:T(8,128)(2,1)} %bitcast.45, bf16[4096,256]{1,0:T(8,128)(2,1)} %bitcast.46, ...), custom_call_target="tpu_custom_call", output_to_operand_aliasing={{0}: (5, {})} | custom-call | tf_op jit(solution)/shard_map/pallas_call | solution.py:167
  162.5 7.2 %all-to-all-start.3 = ((bf16[16,256,256]{2,1,0:T(8,128)(2,1)}), bf16[16,256,256]{2,1,0:T(8,128)(2,1)S(1)}, u32[]{:S(2)}, u32[]{:S(2)}) async-start(bf16[16,256,256]{2,1,0:T(8,128)(2,1)} %bitcast.51), calls=%async_computation.3 | async-start | bytes 4194304 | tf_op jit(solution)/shard_map/all_to_all | solution.py:191
  169.7 1.2 slice.90
  170.9 1.1 slice.89
  172.1 3.5 %collective-permute-start.1 = (bf16[1024,256]{1,0:T(8,128)(2,1)S(1)}, bf16[1024,256]{1,0:T(8,128)(2,1)S(1)}, u32[]{:S(2)}, u32[]{:S(2)}) collective-permute-start(bf16[1024,256]{1,0:T(8,128)(2,1)S(1)} %pad_maximum_fusion.1), channel_id=1, source_target_pairs={{16,0},{32,16},{48,32},{64,48},{80,64},{96,80},{112,96},{17,1},{33... | collective-permute-start | bytes 1572872 | tf_op jit(solution)/shard_map/ppermute | solution.py:21
  177.2 29.4 %collective-permute-done.1 = bf16[1024,256]{1,0:T(8,128)(2,1)S(1)} collective-permute-done((bf16[1024,256]{1,0:T(8,128)(2,1)S(1)}, bf16[1024,256]{1,0:T(8,128)(2,1)S(1)}, u32[]{:S(2)}, u32[]{:S(2)}) %collective-permute-start.1) | collective-permute-done | bytes 524320 | tf_op jit(solution)/shard_map/ppermute | solution.py:21
  206.6 1.0 fusion.4
  207.6 7.2 %all-to-all-start.2 = ((bf16[16,256,256]{2,1,0:T(8,128)(2,1)}), bf16[16,256,256]{2,1,0:T(8,128)(2,1)}, u32[]{:S(2)}, u32[]{:S(2)}) async-start(bf16[16,256,256]{2,1,0:T(8,128)(2,1)} %bitcast.52), calls=%async_computation.2 | async-start | bytes 4194304 | tf_op jit(solution)/shard_map/all_to_all | solution.py:191
  214.9 2.9 %add_convert_fusion = bf16[4096,128]{1,0:T(8,128)(2,1)S(1)} fusion(f32[1024,128]{1,0:T(8,128)} %get-tuple-element.35, f32[1024,128]{1,0:T(8,128)} %slice.66, f32[4096,128]{1,0:T(8,128)} %get-tuple-element.22, f32[4096,128]{1,0:T(8,128)} %get-tuple-element.23), kind=kLoop, calls=%fused_computation.5 | loop fusion | flops 2097152 | bytes 6291456 | tf_op jit(solution)/shard_map/convert_element_type | solution.py:240
  219.1 1.6 pad_maximum_fusion
  220.7 23.3 %all-to-all-done.2 = bf16[16,256,256]{2,1,0:T(8,128)(2,1)} async-done(((bf16[16,256,256]{2,1,0:T(8,128)(2,1)}), bf16[16,256,256]{2,1,0:T(8,128)(2,1)}, u32[]{:S(2)}, u32[]{:S(2)}) %all-to-all-start.2) | async-done | bytes 2097184 | tf_op jit(solution)/shard_map/all_to_all | solution.py:191
  244.0 4.3 %all-to-all-start.4 = ((bf16[16,256,256]{2,1,0:T(8,128)(2,1)}), bf16[16,256,256]{2,1,0:T(8,128)(2,1)}, u32[]{:S(2)}, u32[]{:S(2)}) async-start(bf16[16,256,256]{2,1,0:T(8,128)(2,1)} %bitcast.48), calls=%async_computation.4 | async-start | bytes 4194304 | tf_op jit(solution)/shard_map/all_to_all | solution.py:191
  248.7 1.7 fusion
  250.7 1.6 copy.27
  252.6 1.6 copy.26
  254.2 23.4 %all-to-all-done.4 = bf16[16,256,256]{2,1,0:T(8,128)(2,1)} async-done(((bf16[16,256,256]{2,1,0:T(8,128)(2,1)}), bf16[16,256,256]{2,1,0:T(8,128)(2,1)}, u32[]{:S(2)}, u32[]{:S(2)}) %all-to-all-start.4) | async-done | bytes 2097184 | tf_op jit(solution)/shard_map/all_to_all | solution.py:191
  277.6 1.7 slice_bitcast_fusion
  279.3 1.3 copy.36
  280.5 1.3 copy.37
  (39 shorter events, 7.9 us)
Async XLA Ops:
  0.6 5.6 %copy-start = (bf16[256,2048]{1,0:T(8,128)(2,1)S(1)}, bf16[256,2048]{1,0:T(8,128)(2,1)}, u32[]{:S(2)}) copy-start(bf16[256,2048]{1,0:T(8,128)(2,1)} %param.5) | copy-start | bytes 3145732
  3.3 1.6 copy-start.6
  6.0 1.2 copy-start.9
  10.1 67.3 %all-to-all-start = ((bf16[16,256,512]{2,1,0:T(8,128)(2,1)}), bf16[16,256,512]{2,1,0:T(8,128)(2,1)}, u32[]{:S(2)}, u32[]{:S(2)}) async-start(bf16[16,256,512]{2,1,0:T(8,128)(2,1)} %maximum_bitcast_fusion), calls=%async_computation | async-start | bytes 8388608 | tf_op jit(solution)/shard_map/all_to_all | solution.py:184
  77.3 36.5 %all-to-all-start.1 = ((bf16[16,256,256]{2,1,0:T(8,128)(2,1)}), bf16[16,256,256]{2,1,0:T(8,128)(2,1)S(1)}, u32[]{:S(2)}, u32[]{:S(2)}) async-start(bf16[16,256,256]{2,1,0:T(8,128)(2,1)} %maximum_bitcast_fusion.1), calls=%async_computation.1 | async-start | bytes 4194304 | tf_op jit(solution)/shard_map/all_to_all | solution.py:184
  84.3 36.4 %collective-permute-start = (bf16[1024,256]{1,0:T(8,128)(2,1)S(1)}, bf16[1024,256]{1,0:T(8,128)(2,1)S(1)}, u32[]{:S(2)}, u32[]{:S(2)}) collective-permute-start(bf16[1024,256]{1,0:T(8,128)(2,1)S(1)} %slice.74), channel_id=1, source_target_pairs={{0,16},{16,32},{32,48},{48,64},{64,80},{80,96},{96,112},{1,17},{17... | collective-permute-start | bytes 1572872 | tf_op jit(solution)/shard_map/ppermute | solution.py:21
  113.9 6.9 %copy-start.2 = (bf16[16,256,256]{2,1,0:T(8,128)(2,1)}, bf16[16,256,256]{2,1,0:T(8,128)(2,1)S(1)}, u32[]{:S(2)}) copy-start(bf16[16,256,256]{2,1,0:T(8,128)(2,1)S(1)} %all-to-all-done.1) | copy-start | bytes 6291460
  120.7 0.8 copy-start.8
  162.5 45.2 %all-to-all-start.3 = ((bf16[16,256,256]{2,1,0:T(8,128)(2,1)}), bf16[16,256,256]{2,1,0:T(8,128)(2,1)S(1)}, u32[]{:S(2)}, u32[]{:S(2)}) async-start(bf16[16,256,256]{2,1,0:T(8,128)(2,1)} %bitcast.51), calls=%async_computation.3 | async-start | bytes 4194304 | tf_op jit(solution)/shard_map/all_to_all | solution.py:191
  169.7 5.9 %copy-start.11 = (f32[2048,128]{1,0:T(8,128)S(1)}, f32[2048,128]{1,0:T(8,128)}, u32[]{:S(2)}) copy-start(f32[2048,128]{1,0:T(8,128)} %get-tuple-element.20) | copy-start | bytes 3145732
  169.7 6.7 %copy-start.10 = (f32[2048,128]{1,0:T(8,128)S(1)}, f32[2048,128]{1,0:T(8,128)}, u32[]{:S(2)}) copy-start(f32[2048,128]{1,0:T(8,128)} %get-tuple-element.21) | copy-start | bytes 3145732
  172.1 34.5 %collective-permute-start.1 = (bf16[1024,256]{1,0:T(8,128)(2,1)S(1)}, bf16[1024,256]{1,0:T(8,128)(2,1)S(1)}, u32[]{:S(2)}, u32[]{:S(2)}) collective-permute-start(bf16[1024,256]{1,0:T(8,128)(2,1)S(1)} %pad_maximum_fusion.1), channel_id=1, source_target_pairs={{16,0},{32,16},{48,32},{64,48},{80,64},{96,80},{112,96},{17,1},{33... | collective-permute-start | bytes 1572872 | tf_op jit(solution)/shard_map/ppermute | solution.py:21
  207.6 36.4 %all-to-all-start.2 = ((bf16[16,256,256]{2,1,0:T(8,128)(2,1)}), bf16[16,256,256]{2,1,0:T(8,128)(2,1)}, u32[]{:S(2)}, u32[]{:S(2)}) async-start(bf16[16,256,256]{2,1,0:T(8,128)(2,1)} %bitcast.52), calls=%async_computation.2 | async-start | bytes 4194304 | tf_op jit(solution)/shard_map/all_to_all | solution.py:191
  214.9 3.2 %copy-start.3 = (f32[4096,128]{1,0:T(8,128)S(1)}, f32[4096,128]{1,0:T(8,128)}, u32[]{:S(2)}) copy-start(f32[4096,128]{1,0:T(8,128)} %get-tuple-element.18) | copy-start | bytes 6291460
  214.9 3.8 %copy-start.4 = (f32[4096,128]{1,0:T(8,128)S(1)}, f32[4096,128]{1,0:T(8,128)}, u32[]{:S(2)}) copy-start(f32[4096,128]{1,0:T(8,128)} %get-tuple-element.19) | copy-start | bytes 6291460
  214.9 3.9 %copy-start.5 = (f32[1024,128]{1,0:T(8,128)S(1)}, f32[1024,128]{1,0:T(8,128)}, u32[]{:S(2)}) copy-start(f32[1024,128]{1,0:T(8,128)} %slice.62) | copy-start | bytes 1572868
  214.9 4.0 %copy-start.7 = (f32[1024,128]{1,0:T(8,128)S(1)}, f32[1024,128]{1,0:T(8,128)}, u32[]{:S(2)}) copy-start(f32[1024,128]{1,0:T(8,128)} %get-tuple-element.34) | copy-start | bytes 1572868
  244.0 33.5 %all-to-all-start.4 = ((bf16[16,256,256]{2,1,0:T(8,128)(2,1)}), bf16[16,256,256]{2,1,0:T(8,128)(2,1)}, u32[]{:S(2)}, u32[]{:S(2)}) async-start(bf16[16,256,256]{2,1,0:T(8,128)(2,1)} %bitcast.48), calls=%async_computation.4 | async-start | bytes 4194304 | tf_op jit(solution)/shard_map/all_to_all | solution.py:191
  279.3 2.5 copy-start.1
where the time goes:
time: 284 us; the launch traced here: 282 us
  waiting for transfers between devices  142 us (50%)
  Pallas kernels  65.9 us (23%)
  starting transfers between devices  38.6 us (14%)
  local copies, waits for them, and re-layouts  25 us (9%)
  other arithmetic  9.35 us (3%)
    pallas_call x3, Pallas kernels, attend(): pl.pallas_call(kernel, grid_spec=grid_spec, out_shape=[jax.ShapeDtypeStru...  65.9 us
    all_to_all x2, waiting for transfers between devices, exchange_in(): lax.all_to_all(stacked, 'head', split_axis=0, concat_axis=0, tiled=True)  59.2 us
    all_to_all x3, waiting for transfers between devices, exchange_out(): lax.all_to_all(split, 'head', split_axis=0, concat_axis=0, tiled=True)  46.7 us
    ppermute x2, waiting for transfers between devices, shifted(): return lax.ppermute(block, axis, route)  36.2 us
    all_to_all x3, starting transfers between devices, exchange_out(): lax.all_to_all(split, 'head', split_axis=0, concat_axis=0, tiled=True)  18.8 us
    all_to_all x2, starting transfers between devices, exchange_in(): lax.all_to_all(stacked, 'head', split_axis=0, concat_axis=0, tiled=True)  11.9 us
    unnamed x31, local copies, waits for them, and re-layouts  9.89 us
    ppermute x2, starting transfers between devices, shifted(): return lax.ppermute(block, axis, route)  8.03 us
  transfers between devices with their start and end apart: 7, of which 5 were waited for; matrix products, arithmetic and copies ran while one was open for 7% of the time, Pallas kernels for 9%

commit v1 on v0

--- a/solution.py
+++ b/solution.py
@@ -200,18 +200,17 @@
     grad_rows = grad_out.reshape(token_count, shared, pair)
     key_rows = keys.reshape(token_count, shared, HD)
     value_rows = values.reshape(token_count, shared, HD)
-    first_part = exchange_in(
-        [key_rows, value_rows, query_rows[:, :, :HD], grad_rows[:, :, :HD]]
-    )
+    first_part = exchange_in([key_rows, value_rows])
+    head0_part = exchange_in([query_rows[:, :, :HD], grad_rows[:, :, :HD]])
     second_part = exchange_in([query_rows[:, :, HD:], grad_rows[:, :, HD:]])
     group_rows = first_part.shape[0]
     block_total = group_rows // BLK
     lead = WIN // BLK
     first_query = lax.axis_index("ctx") * group_rows
-    tail = shifted(first_part[group_rows - WIN :, : 2 * HD], "ctx", 1)
+    tail = shifted(first_part[group_rows - WIN :], "ctx", 1)
     late = (lead, block_total - lead)
     early = (0, lead)
-    head0 = (first_part, 2, 3)
+    head0 = (head0_part, 0, 1)
     head1 = (second_part, 0, 1)
     first_out, key_late, value_late = attend([head0], first_part, None, first_query, late, (None,))
     first_out, second_out, key_early, value_early = attend(

time: 284 us -> 260 us (0.915)
  waiting for transfers between devices: 142 us -> 111 us
  local copies, waits for them, and re-layouts: 25 us -> 28.5 us
  starting transfers between devices: 38.6 us -> 42.1 us
    ppermute x2, waiting for transfers between devices: 36.2 us -> 11.6 us  [shifted(): return lax.ppermute(block, axis, route)]
    all_to_all x2 -> x3, waiting for transfers between devices: 59.2 us -> 52.6 us  [exchange_in(): lax.all_to_all(stacked, 'head', split_axis=0, concat_axis=0, tiled=True)]
    all_to_all x2 -> x3, starting transfers between devices: 11.9 us -> 15.3 us  [exchange_in(): lax.all_to_all(stacked, 'head', split_axis=0, concat_axis=0, tiled=True)]
    unnamed x31 -> x35, local copies, waits for them, and re-layouts: 9.89 us -> 11.3 us
  transfers between devices with their start and end apart: 7 -> 8, of which waited for: 5 -> 7; matrix products, arithmetic and copies ran while one was open for 7% -> 8% of each run, Pallas kernels for 9% -> 19%
where the time goes in v1:
time: 260 us; the launch traced here: 258 us
  waiting for transfers between devices  111 us (43%)
  Pallas kernels  65.7 us (25%)
  starting transfers between devices  42.1 us (16%)
  local copies, waits for them, and re-layouts  28.5 us (11%)
  other arithmetic  10.2 us (4%)
    pallas_call x3, Pallas kernels, attend(): pl.pallas_call(kernel, grid_spec=grid_spec, out_shape=[jax.ShapeDtypeStru...  65.7 us
    all_to_all x3, waiting for transfers between devices, exchange_in(): lax.all_to_all(stacked, 'head', split_axis=0, concat_axis=0, tiled=True)  52.6 us
    all_to_all x3, waiting for transfers between devices, exchange_out(): lax.all_to_all(split, 'head', split_axis=0, concat_axis=0, tiled=True)  46.7 us
    all_to_all x3, starting transfers between devices, exchange_out(): lax.all_to_all(split, 'head', split_axis=0, concat_axis=0, tiled=True)  18.8 us
    all_to_all x3, starting transfers between devices, exchange_in(): lax.all_to_all(stacked, 'head', split_axis=0, concat_axis=0, tiled=True)  15.3 us
    ppermute x2, waiting for transfers between devices, shifted(): return lax.ppermute(block, axis, route)  11.6 us
    unnamed x35, local copies, waits for them, and re-layouts  11.3 us
    ppermute x2, starting transfers between devices, shifted(): return lax.ppermute(block, axis, route)  8.04 us
  transfers between devices with their start and end apart: 8, of which 7 were waited for; matrix products, arithmetic and copies ran while one was open for 8% of the time, Pallas kernels for 19%

profile of v1, /device:TPU:121, one launch (start us, length us, event | category | flops | bytes accessed | tf_op | source)
XLA Modules:
  0.0 258.4 jit_solution(1354397886191089648)
XLA Ops:
  0.6 2.3 copy.30
  3.0 1.3 fusion.2
  4.6 1.3 copy-done.10
  6.5 1.3 fusion.3
  8.2 1.6 maximum_bitcast_fusion
  9.8 5.9 %all-to-all-start = ((bf16[16,256,256]{2,1,0:T(8,128)(2,1)}), bf16[16,256,256]{2,1,0:T(8,128)(2,1)S(1)}, u32[]{:S(2)}, u32[]{:S(2)}) async-start(bf16[16,256,256]{2,1,0:T(8,128)(2,1)} %maximum_bitcast_fusion), calls=%async_computation | async-start | bytes 4194304 | tf_op jit(solution)/shard_map/all_to_all | solution.py:184
  15.7 1.8 copy_bitcast_fusion.2
  17.5 1.6 maximum_bitcast_fusion.2
  19.1 25.8 %all-to-all-done = bf16[16,256,256]{2,1,0:T(8,128)(2,1)S(1)} async-done(((bf16[16,256,256]{2,1,0:T(8,128)(2,1)}), bf16[16,256,256]{2,1,0:T(8,128)(2,1)S(1)}, u32[]{:S(2)}, u32[]{:S(2)}) %all-to-all-start) | async-done | bytes 2097184 | tf_op jit(solution)/shard_map/all_to_all | solution.py:184
  44.9 1.4 copy-done.3
  46.3 4.7 %all-to-all-start.2 = ((bf16[16,256,256]{2,1,0:T(8,128)(2,1)}), bf16[16,256,256]{2,1,0:T(8,128)(2,1)S(1)}, u32[]{:S(2)}, u32[]{:S(2)}) async-start(bf16[16,256,256]{2,1,0:T(8,128)(2,1)} %maximum_bitcast_fusion.2), calls=%async_computation.2 | async-start | bytes 4194304 | tf_op jit(solution)/shard_map/all_to_all | solution.py:184
  52.4 1.6 maximum_bitcast_fusion.1
  54.1 26.1 %all-to-all-done.2 = bf16[16,256,256]{2,1,0:T(8,128)(2,1)S(1)} async-done(((bf16[16,256,256]{2,1,0:T(8,128)(2,1)}), bf16[16,256,256]{2,1,0:T(8,128)(2,1)S(1)}, u32[]{:S(2)}, u32[]{:S(2)}) %all-to-all-start.2) | async-done | bytes 2097184 | tf_op jit(solution)/shard_map/all_to_all | solution.py:184
  80.1 4.7 %all-to-all-start.1 = ((bf16[16,256,256]{2,1,0:T(8,128)(2,1)}), bf16[16,256,256]{2,1,0:T(8,128)(2,1)}, u32[]{:S(2)}, u32[]{:S(2)}) async-start(bf16[16,256,256]{2,1,0:T(8,128)(2,1)} %maximum_bitcast_fusion.1), calls=%async_computation.1 | async-start | bytes 4194304 | tf_op jit(solution)/shard_map/all_to_all | solution.py:184
  84.9 4.4 %collective-permute-start = (bf16[1024,256]{1,0:T(8,128)(2,1)S(1)}, bf16[1024,256]{1,0:T(8,128)(2,1)S(1)}, u32[]{:S(2)}, u32[]{:S(2)}) collective-permute-start(bf16[1024,256]{1,0:T(8,128)(2,1)S(1)} %bitcast.69), channel_id=1, source_target_pairs={{0,16},{16,32},{32,48},{48,64},{64,80},{80,96},{96,112},{1,17},{17... | collective-permute-start | bytes 1572872 | tf_op jit(solution)/shard_map/ppermute | solution.py:21
  89.2 24.8 %shard_map.75 = (bf16[4096,256]{1,0:T(8,128)(2,1)}, f32[4096,128]{1,0:T(8,128)}, f32[4096,128]{1,0:T(8,128)}) custom-call(s32[1]{0:T(128)} %bitcast.first_ref, bf16[4096,256]{1,0:T(8,128)(2,1)} %bitcast.53, bf16[4096,256]{1,0:T(8,128)(2,1)} %bitcast.54, bf16[4096,256]{1,0:T(8,128)(2,1)} %bitcast.47, bf16[4096,256]{1,0:T(8,128)(2,1)} %bitcast.48), custom_call_target="tpu_custom_call" | custom-call | tf_op jit(solution)/shard_map/pallas_call | solution.py:167
  114.8 7.4 %collective-permute-done.refs_4_.refs_5_ = bf16[1024,256]{1,0:T(8,128)(2,1)S(1)} collective-permute-done((bf16[1024,256]{1,0:T(8,128)(2,1)S(1)}, bf16[1024,256]{1,0:T(8,128)(2,1)S(1)}, u32[]{:S(2)}, u32[]{:S(2)}) %collective-permute-start) | collective-permute-done | bytes 524320 | tf_op jit(solution)/shard_map/ppermute | solution.py:21
  123.1 16.0 %shard_map.76 = (bf16[4096,256]{1,0:T(8,128)(2,1)}, bf16[4096,256]{1,0:T(8,128)(2,1)}, f32[2048,128]{1,0:T(8,128)}, f32[2048,128]{1,0:T(8,128)}) custom-call(s32[1]{0:T(128)} %bitcast.first_ref, bf16[4096,256]{1,0:T(8,128)(2,1)} %bitcast.55, bf16[4096,256]{1,0:T(8,128)(2,1)} %bitcast.56, ...), custom_call_target="tpu_custom_call", output_to_operand_aliasing={{0}: (9, {})} | custom-call | tf_op jit(solution)/shard_map/pallas_call | solution.py:167
  139.1 7.3 %all-to-all-start.3 = ((bf16[16,256,256]{2,1,0:T(8,128)(2,1)}), bf16[16,256,256]{2,1,0:T(8,128)(2,1)S(1)}, u32[]{:S(2)}, u32[]{:S(2)}) async-start(bf16[16,256,256]{2,1,0:T(8,128)(2,1)} %bitcast.57), calls=%async_computation.3 | async-start | bytes 4194304 | tf_op jit(solution)/shard_map/all_to_all | solution.py:191
  148.7 3.7 %collective-permute-start.1 = (bf16[1024,256]{1,0:T(8,128)(2,1)S(1)}, bf16[1024,256]{1,0:T(8,128)(2,1)S(1)}, u32[]{:S(2)}, u32[]{:S(2)}) collective-permute-start(bf16[1024,256]{1,0:T(8,128)(2,1)S(1)} %pad_maximum_fusion.1), channel_id=1, source_target_pairs={{16,0},{32,16},{48,32},{64,48},{80,64},{96,80},{112,96},{17,1},{33... | collective-permute-start | bytes 1572872 | tf_op jit(solution)/shard_map/ppermute | solution.py:21
  154.1 24.9 %shard_map.77 = (bf16[4096,256]{1,0:T(8,128)(2,1)}, f32[4096,128]{1,0:T(8,128)}, f32[4096,128]{1,0:T(8,128)}) custom-call(s32[1]{0:T(128)} %bitcast.first_ref, bf16[4096,256]{1,0:T(8,128)(2,1)} %bitcast.4.refs_2_.refs_3_.refs_0_.refs_1_, bf16[4096,256]{1,0:T(8,128)(2,1)} %bitcast.4.refs_2_.refs_3_.refs_0_.refs_1_, ...), custom_call_target="tpu_custom_call", output_to_operand_aliasing={{0}: (5, {})} | custom-call | tf_op jit(solution)/shard_map/pallas_call | solution.py:167
  179.0 4.2 %collective-permute-done.1 = bf16[1024,256]{1,0:T(8,128)(2,1)S(1)} collective-permute-done((bf16[1024,256]{1,0:T(8,128)(2,1)S(1)}, bf16[1024,256]{1,0:T(8,128)(2,1)S(1)}, u32[]{:S(2)}, u32[]{:S(2)}) %collective-permute-start.1) | collective-permute-done | bytes 524320 | tf_op jit(solution)/shard_map/ppermute | solution.py:21
  184.3 7.2 %all-to-all-start.4 = ((bf16[16,256,256]{2,1,0:T(8,128)(2,1)}), bf16[16,256,256]{2,1,0:T(8,128)(2,1)}, u32[]{:S(2)}, u32[]{:S(2)}) async-start(bf16[16,256,256]{2,1,0:T(8,128)(2,1)} %bitcast.62), calls=%async_computation.4 | async-start | bytes 4194304 | tf_op jit(solution)/shard_map/all_to_all | solution.py:191
  191.5 2.9 %add_convert_fusion = bf16[4096,128]{1,0:T(8,128)(2,1)S(1)} fusion(f32[1024,128]{1,0:T(8,128)} %get-tuple-element.35, f32[1024,128]{1,0:T(8,128)} %slice.70, f32[4096,128]{1,0:T(8,128)} %get-tuple-element.22, f32[4096,128]{1,0:T(8,128)} %get-tuple-element.23), kind=kLoop, calls=%fused_computation.6 | loop fusion | flops 2097152 | bytes 6291456 | tf_op jit(solution)/shard_map/convert_element_type | solution.py:239
  195.8 1.6 pad_maximum_fusion
  197.3 23.3 %all-to-all-done.4 = bf16[16,256,256]{2,1,0:T(8,128)(2,1)} async-done(((bf16[16,256,256]{2,1,0:T(8,128)(2,1)}), bf16[16,256,256]{2,1,0:T(8,128)(2,1)}, u32[]{:S(2)}, u32[]{:S(2)}) %all-to-all-start.4) | async-done | bytes 2097184 | tf_op jit(solution)/shard_map/all_to_all | solution.py:191
  220.7 4.3 %all-to-all-start.5 = ((bf16[16,256,256]{2,1,0:T(8,128)(2,1)}), bf16[16,256,256]{2,1,0:T(8,128)(2,1)}, u32[]{:S(2)}, u32[]{:S(2)}) async-start(bf16[16,256,256]{2,1,0:T(8,128)(2,1)} %bitcast.59), calls=%async_computation.5 | async-start | bytes 4194304 | tf_op jit(solution)/shard_map/all_to_all | solution.py:191
  225.4 1.7 fusion.1
  227.4 1.6 copy.27
  229.2 1.6 copy.26
  230.8 23.4 %all-to-all-done.5 = bf16[16,256,256]{2,1,0:T(8,128)(2,1)} async-done(((bf16[16,256,256]{2,1,0:T(8,128)(2,1)}), bf16[16,256,256]{2,1,0:T(8,128)(2,1)}, u32[]{:S(2)}, u32[]{:S(2)}) %all-to-all-start.5) | async-done | bytes 2097184 | tf_op jit(solution)/shard_map/all_to_all | solution.py:191
  254.2 1.7 slice_bitcast_fusion
  (46 shorter events, 14.2 us)
Async XLA Ops:
  0.6 15.1 %copy-start = (bf16[256,2048]{1,0:T(8,128)(2,1)S(1)}, bf16[256,2048]{1,0:T(8,128)(2,1)}, u32[]{:S(2)}) copy-start(bf16[256,2048]{1,0:T(8,128)(2,1)} %param.5) | copy-start | bytes 3145732
  4.3 1.6 copy-start.10
  9.8 35.1 %all-to-all-start = ((bf16[16,256,256]{2,1,0:T(8,128)(2,1)}), bf16[16,256,256]{2,1,0:T(8,128)(2,1)S(1)}, u32[]{:S(2)}, u32[]{:S(2)}) async-start(bf16[16,256,256]{2,1,0:T(8,128)(2,1)} %maximum_bitcast_fusion), calls=%async_computation | async-start | bytes 4194304 | tf_op jit(solution)/shard_map/all_to_all | solution.py:184
  19.1 31.8 %copy-start.4 = (bf16[256,16,128]{2,1,0:T(8,128)(2,1)S(1)}, bf16[256,16,128]{2,1,0:T(8,128)(2,1)}, u32[]{:S(2)}) copy-start(bf16[256,16,128]{2,1,0:T(8,128)(2,1)} %get-tuple-element.31) | copy-start | bytes 3145732
  44.9 1.4 copy-start.3
  46.3 33.9 %all-to-all-start.2 = ((bf16[16,256,256]{2,1,0:T(8,128)(2,1)}), bf16[16,256,256]{2,1,0:T(8,128)(2,1)S(1)}, u32[]{:S(2)}, u32[]{:S(2)}) async-start(bf16[16,256,256]{2,1,0:T(8,128)(2,1)} %maximum_bitcast_fusion.2), calls=%async_computation.2 | async-start | bytes 4194304 | tf_op jit(solution)/shard_map/all_to_all | solution.py:184
  50.9 1.2 copy-start.5
  80.1 4.7 %copy-start.2 = (bf16[16,256,256]{2,1,0:T(8,128)(2,1)}, bf16[16,256,256]{2,1,0:T(8,128)(2,1)S(1)}, u32[]{:S(2)}) copy-start(bf16[16,256,256]{2,1,0:T(8,128)(2,1)S(1)} %all-to-all-done.2) | copy-start | bytes 6291460
  80.1 34.7 %all-to-all-start.1 = ((bf16[16,256,256]{2,1,0:T(8,128)(2,1)}), bf16[16,256,256]{2,1,0:T(8,128)(2,1)}, u32[]{:S(2)}, u32[]{:S(2)}) async-start(bf16[16,256,256]{2,1,0:T(8,128)(2,1)} %maximum_bitcast_fusion.1), calls=%async_computation.1 | async-start | bytes 4194304 | tf_op jit(solution)/shard_map/all_to_all | solution.py:184
  84.9 37.4 %collective-permute-start = (bf16[1024,256]{1,0:T(8,128)(2,1)S(1)}, bf16[1024,256]{1,0:T(8,128)(2,1)S(1)}, u32[]{:S(2)}, u32[]{:S(2)}) collective-permute-start(bf16[1024,256]{1,0:T(8,128)(2,1)S(1)} %bitcast.69), channel_id=1, source_target_pairs={{0,16},{16,32},{32,48},{48,64},{64,80},{80,96},{96,112},{1,17},{17... | collective-permute-start | bytes 1572872 | tf_op jit(solution)/shard_map/ppermute | solution.py:21
  122.2 0.8 copy-start.8
  139.1 45.2 %all-to-all-start.3 = ((bf16[16,256,256]{2,1,0:T(8,128)(2,1)}), bf16[16,256,256]{2,1,0:T(8,128)(2,1)S(1)}, u32[]{:S(2)}, u32[]{:S(2)}) async-start(bf16[16,256,256]{2,1,0:T(8,128)(2,1)} %bitcast.57), calls=%async_computation.3 | async-start | bytes 4194304 | tf_op jit(solution)/shard_map/all_to_all | solution.py:191
  146.3 6.1 %copy-start.13 = (f32[2048,128]{1,0:T(8,128)S(1)}, f32[2048,128]{1,0:T(8,128)}, u32[]{:S(2)}) copy-start(f32[2048,128]{1,0:T(8,128)} %get-tuple-element.20) | copy-start | bytes 3145732
  146.3 6.9 %copy-start.12 = (f32[2048,128]{1,0:T(8,128)S(1)}, f32[2048,128]{1,0:T(8,128)}, u32[]{:S(2)}) copy-start(f32[2048,128]{1,0:T(8,128)} %get-tuple-element.21) | copy-start | bytes 3145732
  148.7 34.5 %collective-permute-start.1 = (bf16[1024,256]{1,0:T(8,128)(2,1)S(1)}, bf16[1024,256]{1,0:T(8,128)(2,1)S(1)}, u32[]{:S(2)}, u32[]{:S(2)}) collective-permute-start(bf16[1024,256]{1,0:T(8,128)(2,1)S(1)} %pad_maximum_fusion.1), channel_id=1, source_target_pairs={{16,0},{32,16},{48,32},{64,48},{80,64},{96,80},{112,96},{17,1},{33... | collective-permute-start | bytes 1572872 | tf_op jit(solution)/shard_map/ppermute | solution.py:21
  184.3 36.4 %all-to-all-start.4 = ((bf16[16,256,256]{2,1,0:T(8,128)(2,1)}), bf16[16,256,256]{2,1,0:T(8,128)(2,1)}, u32[]{:S(2)}, u32[]{:S(2)}) async-start(bf16[16,256,256]{2,1,0:T(8,128)(2,1)} %bitcast.62), calls=%async_computation.4 | async-start | bytes 4194304 | tf_op jit(solution)/shard_map/all_to_all | solution.py:191
  191.5 3.2 %copy-start.6 = (f32[4096,128]{1,0:T(8,128)S(1)}, f32[4096,128]{1,0:T(8,128)}, u32[]{:S(2)}) copy-start(f32[4096,128]{1,0:T(8,128)} %get-tuple-element.18) | copy-start | bytes 6291460
  191.5 3.8 %copy-start.7 = (f32[4096,128]{1,0:T(8,128)S(1)}, f32[4096,128]{1,0:T(8,128)}, u32[]{:S(2)}) copy-start(f32[4096,128]{1,0:T(8,128)} %get-tuple-element.19) | copy-start | bytes 6291460
  191.5 3.9 %copy-start.9 = (f32[1024,128]{1,0:T(8,128)S(1)}, f32[1024,128]{1,0:T(8,128)}, u32[]{:S(2)}) copy-start(f32[1024,128]{1,0:T(8,128)} %slice.66) | copy-start | bytes 1572868
  191.5 4.0 %copy-start.11 = (f32[1024,128]{1,0:T(8,128)S(1)}, f32[1024,128]{1,0:T(8,128)}, u32[]{:S(2)}) copy-start(f32[1024,128]{1,0:T(8,128)} %get-tuple-element.34) | copy-start | bytes 1572868
  220.7 33.5 %all-to-all-start.5 = ((bf16[16,256,256]{2,1,0:T(8,128)(2,1)}), bf16[16,256,256]{2,1,0:T(8,128)(2,1)}, u32[]{:S(2)}, u32[]{:S(2)}) async-start(bf16[16,256,256]{2,1,0:T(8,128)(2,1)} %bitcast.59), calls=%async_computation.5 | async-start | bytes 4194304 | tf_op jit(solution)/shard_map/all_to_all | solution.py:191
  255.9 2.5 copy-start.1

commit v2 on v0

--- a/solution.py
+++ b/solution.py
@@ -37,8 +37,13 @@
     pos += sum(carry_od)
     od_refs = refs[pos : pos + heads]
     pos += heads
-    dk_ref, dv_ref, bias_ref = refs[pos : pos + 3]
-    pos += 3
+    dk_ref, dv_ref = refs[pos : pos + 2]
+    pos += 2
+    if early:
+        halo_ref = refs[pos]
+        pos += 1
+    bias_ref = refs[pos]
+    pos += 1
     if early:
         kx_ref, vx_ref = refs[pos : pos + 2]
     step = pl.program_id(0)
@@ -102,6 +107,12 @@
     acc_start = pl.multiple_of(start - acc_base, rows)
     dk_ref[pl.ds(acc_start, span), :] += dk_acc
     dv_ref[pl.ds(acc_start, span), :] += dv_acc
+    if early:
+
+        @pl.when(step == pl.num_programs(0) - 1)
+        def _():
+            halo_ref[:, :HD] = dk_ref[:WIN, :].astype(jnp.bfloat16)
+            halo_ref[:, HD:] = dv_ref[:WIN, :].astype(jnp.bfloat16)
 
 
 def attend(sources, first_part, tail, first_query, blocks, carried_od):
@@ -153,7 +164,8 @@
         grid=(block_count,),
         in_specs=in_specs,
         out_specs=[pl.BlockSpec((rows, 2 * HD), lambda b, f: (b + block_offset, 0))] * heads
-        + [whole, whole],
+        + [whole, whole]
+        + ([pl.BlockSpec((WIN, 2 * HD), lambda b, f: (0, 0))] if early else []),
         scratch_shapes=scratch,
     )
     kernel = functools.partial(
@@ -171,7 +183,8 @@
         + [
             jax.ShapeDtypeStruct((acc_rows, HD), jnp.float32),
             jax.ShapeDtypeStruct((acc_rows, HD), jnp.float32),
-        ],
+        ]
+        + ([jax.ShapeDtypeStruct((WIN, 2 * HD), jnp.bfloat16)] if early else []),
         input_output_aliases=aliases,
         compiler_params=pltpu.CompilerParams(
             dimension_semantics=("arbitrary",), vmem_limit_bytes=56 * 1024 * 1024
@@ -214,14 +227,10 @@
     head0 = (first_part, 2, 3)
     head1 = (second_part, 0, 1)
     first_out, key_late, value_late = attend([head0], first_part, None, first_query, late, (None,))
-    first_out, second_out, key_early, value_early = attend(
+    first_out, second_out, key_early, value_early, halo_part = attend(
         [head0, head1], first_part, tail, first_query, early, (first_out, None)
     )
-    back = shifted(
-        jnp.concatenate([key_early[:WIN], value_early[:WIN]], axis=1).astype(jnp.bfloat16),
-        "ctx",
-        -1,
-    ).astype(jnp.float32)
+    back = shifted(halo_part, "ctx", -1).astype(jnp.float32)
     second_out, key_last, value_last = attend(
         [head1], first_part, None, first_query, late, (second_out,)
     )

time: 284 us -> 284 us (level)
    unnamed x31 -> x29, local copies, waits for them, and re-layouts: 9.89 us -> 9.91 us
where the time goes in v2:
time: 284 us; the launch traced here: 282 us
  waiting for transfers between devices  142 us (50%)
  Pallas kernels  66.3 us (23%)
  starting transfers between devices  38.8 us (14%)
  local copies, waits for them, and re-layouts  24.8 us (9%)
  other arithmetic  9.27 us (3%)
    pallas_call x3, Pallas kernels, attend(): pl.pallas_call(kernel, grid_spec=grid_spec, out_shape=[jax.ShapeDtypeStru...  66.3 us
    all_to_all x2, waiting for transfers between devices, exchange_in(): lax.all_to_all(stacked, 'head', split_axis=0, concat_axis=0, tiled=True)  59.2 us
    all_to_all x3, waiting for transfers between devices, exchange_out(): lax.all_to_all(split, 'head', split_axis=0, concat_axis=0, tiled=True)  46.7 us
    ppermute x2, waiting for transfers between devices, shifted(): return lax.ppermute(block, axis, route)  36.5 us
    all_to_all x3, starting transfers between devices, exchange_out(): lax.all_to_all(split, 'head', split_axis=0, concat_axis=0, tiled=True)  18.9 us
    all_to_all x2, starting transfers between devices, exchange_in(): lax.all_to_all(stacked, 'head', split_axis=0, concat_axis=0, tiled=True)  11.9 us
    unnamed x29, local copies, waits for them, and re-layouts  9.91 us
    ppermute x2, starting transfers between devices, shifted(): return lax.ppermute(block, axis, route)  8.05 us
  transfers between devices with their start and end apart: 7, of which 5 were waited for; matrix products, arithmetic and copies ran while one was open for 7% of the time, Pallas kernels for 9%

profile of v2, /device:TPU:121, one launch (start us, length us, event | category | flops | bytes accessed | tf_op | source)
XLA Modules:
  0.0 282.4 jit_solution(5497950791801424674)
XLA Ops:
  0.6 2.3 copy.30
  3.6 1.3 copy-done.6
  6.3 0.9 copy-done.9
  7.7 2.3 maximum_bitcast_fusion
  10.0 5.9 %all-to-all-start = ((bf16[16,256,512]{2,1,0:T(8,128)(2,1)}), bf16[16,256,512]{2,1,0:T(8,128)(2,1)}, u32[]{:S(2)}, u32[]{:S(2)}) async-start(bf16[16,256,512]{2,1,0:T(8,128)(2,1)} %maximum_bitcast_fusion), calls=%async_computation | async-start | bytes 8388608 | tf_op jit(solution)/shard_map/all_to_all | solution.py:197
  16.5 1.6 maximum_bitcast_fusion.1
  18.1 59.2 %all-to-all-done = bf16[16,256,512]{2,1,0:T(8,128)(2,1)} async-done(((bf16[16,256,512]{2,1,0:T(8,128)(2,1)}), bf16[16,256,512]{2,1,0:T(8,128)(2,1)}, u32[]{:S(2)}, u32[]{:S(2)}) %all-to-all-start) | async-done | bytes 4194336 | tf_op jit(solution)/shard_map/all_to_all | solution.py:197
  77.3 5.9 %all-to-all-start.1 = ((bf16[16,256,256]{2,1,0:T(8,128)(2,1)}), bf16[16,256,256]{2,1,0:T(8,128)(2,1)S(1)}, u32[]{:S(2)}, u32[]{:S(2)}) async-start(bf16[16,256,256]{2,1,0:T(8,128)(2,1)} %maximum_bitcast_fusion.1), calls=%async_computation.1 | async-start | bytes 4194304 | tf_op jit(solution)/shard_map/all_to_all | solution.py:197
  83.2 1.1 slice.64
  84.3 4.5 %collective-permute-start = (bf16[1024,256]{1,0:T(8,128)(2,1)S(1)}, bf16[1024,256]{1,0:T(8,128)(2,1)S(1)}, u32[]{:S(2)}, u32[]{:S(2)}) collective-permute-start(bf16[1024,256]{1,0:T(8,128)(2,1)S(1)} %slice.64), channel_id=1, source_target_pairs={{0,16},{16,32},{32,48},{48,64},{64,80},{80,96},{96,112},{1,17},{17... | collective-permute-start | bytes 1572872 | tf_op jit(solution)/shard_map/ppermute | solution.py:21
  88.9 25.0 %shard_map.75 = (bf16[4096,256]{1,0:T(8,128)(2,1)}, f32[4096,128]{1,0:T(8,128)}, f32[4096,128]{1,0:T(8,128)}) custom-call(s32[1]{0:T(128)} %bitcast.first_ref, bf16[4096,512]{1,0:T(8,128)(2,1)} %bitcast.2.refs_0_.refs_1_.refs_2_.refs_3_.refs_6_.refs_7_, bf16[4096,512]{1,0:T(8,128)(2,1)} %bitcast.2.refs_0_.refs_1_.refs_2_.refs_3_.refs_6_.refs_7_, ...), custom_call_target="tpu_custom_call" | custom-call | tf_op jit(solution)/shard_map/pallas_call | solution.py:179
  113.9 6.8 %collective-permute-done.refs_4_.refs_5_ = bf16[1024,256]{1,0:T(8,128)(2,1)S(1)} collective-permute-done((bf16[1024,256]{1,0:T(8,128)(2,1)S(1)}, bf16[1024,256]{1,0:T(8,128)(2,1)S(1)}, u32[]{:S(2)}, u32[]{:S(2)}) %collective-permute-start) | collective-permute-done | bytes 524320 | tf_op jit(solution)/shard_map/ppermute | solution.py:21
  121.6 16.5 %shard_map.76 = (bf16[4096,256]{1,0:T(8,128)(2,1)}, bf16[4096,256]{1,0:T(8,128)(2,1)}, f32[2048,128]{1,0:T(8,128)}, f32[2048,128]{1,0:T(8,128)}, bf16[1024,256]{1,0:T(8,128)(2,1)}) custom-call(s32[1]{0:T(128)} %bitcast.first_ref, bf16[4096,512]{1,0:T(8,128)(2,1)} %bitcast.2.refs_0_.refs_1_.refs_2_.refs_3_.refs_6_.refs_7_, ...), custom_call_target="tpu_custom_call", output_to_operand_aliasing={{0}: (9, {})} | custom-call | tf_op jit(solution)/shard_map/pallas_call | solution.py:179
  138.0 24.9 %shard_map.77 = (bf16[4096,256]{1,0:T(8,128)(2,1)}, f32[4096,128]{1,0:T(8,128)}, f32[4096,128]{1,0:T(8,128)}) custom-call(s32[1]{0:T(128)} %bitcast.first_ref, bf16[4096,256]{1,0:T(8,128)(2,1)} %bitcast.45, bf16[4096,256]{1,0:T(8,128)(2,1)} %bitcast.46, ...), custom_call_target="tpu_custom_call", output_to_operand_aliasing={{0}: (5, {})} | custom-call | tf_op jit(solution)/shard_map/pallas_call | solution.py:179
  162.9 7.4 %all-to-all-start.3 = ((bf16[16,256,256]{2,1,0:T(8,128)(2,1)}), bf16[16,256,256]{2,1,0:T(8,128)(2,1)S(1)}, u32[]{:S(2)}, u32[]{:S(2)}) async-start(bf16[16,256,256]{2,1,0:T(8,128)(2,1)} %bitcast.51), calls=%async_computation.3 | async-start | bytes 4194304 | tf_op jit(solution)/shard_map/all_to_all | solution.py:204
  170.3 3.5 %collective-permute-start.1 = (bf16[1024,256]{1,0:T(8,128)(2,1)S(1)}, bf16[1024,256]{1,0:T(8,128)(2,1)S(1)}, u32[]{:S(2)}, u32[]{:S(2)}) collective-permute-start(bf16[1024,256]{1,0:T(8,128)(2,1)S(1)} %copy-done.10), channel_id=1, source_target_pairs={{16,0},{32,16},{48,32},{64,48},{80,64},{96,80},{112,96},{17,1},{33... | collective-permute-start | bytes 1572872 | tf_op jit(solution)/shard_map/ppermute | solution.py:21
  173.8 1.9 slice.54
  175.7 1.9 slice.56
  177.6 29.6 %collective-permute-done.1 = bf16[1024,256]{1,0:T(8,128)(2,1)S(1)} collective-permute-done((bf16[1024,256]{1,0:T(8,128)(2,1)S(1)}, bf16[1024,256]{1,0:T(8,128)(2,1)S(1)}, u32[]{:S(2)}, u32[]{:S(2)}) %collective-permute-start.1) | collective-permute-done | bytes 524320 | tf_op jit(solution)/shard_map/ppermute | solution.py:21
  207.2 1.0 fusion.4
  208.2 7.2 %all-to-all-start.2 = ((bf16[16,256,256]{2,1,0:T(8,128)(2,1)}), bf16[16,256,256]{2,1,0:T(8,128)(2,1)}, u32[]{:S(2)}, u32[]{:S(2)}) async-start(bf16[16,256,256]{2,1,0:T(8,128)(2,1)} %bitcast.52), calls=%async_computation.2 | async-start | bytes 4194304 | tf_op jit(solution)/shard_map/all_to_all | solution.py:204
  215.5 2.9 %add_convert_fusion = bf16[4096,128]{1,0:T(8,128)(2,1)S(1)} fusion(f32[1024,128]{1,0:T(8,128)} %get-tuple-element.37, f32[1024,128]{1,0:T(8,128)} %slice.56, f32[4096,128]{1,0:T(8,128)} %get-tuple-element.23, f32[4096,128]{1,0:T(8,128)} %get-tuple-element.24), kind=kLoop, calls=%fused_computation.5 | loop fusion | flops 2097152 | bytes 6291456 | tf_op jit(solution)/shard_map/convert_element_type | solution.py:249
  219.7 1.6 pad_maximum_fusion
  221.3 23.3 %all-to-all-done.2 = bf16[16,256,256]{2,1,0:T(8,128)(2,1)} async-done(((bf16[16,256,256]{2,1,0:T(8,128)(2,1)}), bf16[16,256,256]{2,1,0:T(8,128)(2,1)}, u32[]{:S(2)}, u32[]{:S(2)}) %all-to-all-start.2) | async-done | bytes 2097184 | tf_op jit(solution)/shard_map/all_to_all | solution.py:204
  244.6 4.3 %all-to-all-start.4 = ((bf16[16,256,256]{2,1,0:T(8,128)(2,1)}), bf16[16,256,256]{2,1,0:T(8,128)(2,1)}, u32[]{:S(2)}, u32[]{:S(2)}) async-start(bf16[16,256,256]{2,1,0:T(8,128)(2,1)} %bitcast.48), calls=%async_computation.4 | async-start | bytes 4194304 | tf_op jit(solution)/shard_map/all_to_all | solution.py:204
  249.4 1.7 fusion
  251.4 1.6 copy.27
  253.2 1.6 copy.26
  254.8 23.4 %all-to-all-done.4 = bf16[16,256,256]{2,1,0:T(8,128)(2,1)} async-done(((bf16[16,256,256]{2,1,0:T(8,128)(2,1)}), bf16[16,256,256]{2,1,0:T(8,128)(2,1)}, u32[]{:S(2)}, u32[]{:S(2)}) %all-to-all-start.4) | async-done | bytes 2097184 | tf_op jit(solution)/shard_map/all_to_all | solution.py:204
  278.2 1.7 slice_bitcast_fusion
  279.9 1.3 copy.36
  281.1 1.3 copy.37
  (34 shorter events, 6.1 us)
Async XLA Ops:
  0.6 5.6 %copy-start = (bf16[256,2048]{1,0:T(8,128)(2,1)S(1)}, bf16[256,2048]{1,0:T(8,128)(2,1)}, u32[]{:S(2)}) copy-start(bf16[256,2048]{1,0:T(8,128)(2,1)} %param.5) | copy-start | bytes 3145732
  3.3 1.6 copy-start.6
  6.0 1.2 copy-start.9
  10.0 67.3 %all-to-all-start = ((bf16[16,256,512]{2,1,0:T(8,128)(2,1)}), bf16[16,256,512]{2,1,0:T(8,128)(2,1)}, u32[]{:S(2)}, u32[]{:S(2)}) async-start(bf16[16,256,512]{2,1,0:T(8,128)(2,1)} %maximum_bitcast_fusion), calls=%async_computation | async-start | bytes 8388608 | tf_op jit(solution)/shard_map/all_to_all | solution.py:197
  77.3 36.5 %all-to-all-start.1 = ((bf16[16,256,256]{2,1,0:T(8,128)(2,1)}), bf16[16,256,256]{2,1,0:T(8,128)(2,1)S(1)}, u32[]{:S(2)}, u32[]{:S(2)}) async-start(bf16[16,256,256]{2,1,0:T(8,128)(2,1)} %maximum_bitcast_fusion.1), calls=%async_computation.1 | async-start | bytes 4194304 | tf_op jit(solution)/shard_map/all_to_all | solution.py:197
  84.3 36.4 %collective-permute-start = (bf16[1024,256]{1,0:T(8,128)(2,1)S(1)}, bf16[1024,256]{1,0:T(8,128)(2,1)S(1)}, u32[]{:S(2)}, u32[]{:S(2)}) collective-permute-start(bf16[1024,256]{1,0:T(8,128)(2,1)S(1)} %slice.64), channel_id=1, source_target_pairs={{0,16},{16,32},{32,48},{48,64},{64,80},{80,96},{96,112},{1,17},{17... | collective-permute-start | bytes 1572872 | tf_op jit(solution)/shard_map/ppermute | solution.py:21
  113.8 6.9 %copy-start.2 = (bf16[16,256,256]{2,1,0:T(8,128)(2,1)}, bf16[16,256,256]{2,1,0:T(8,128)(2,1)S(1)}, u32[]{:S(2)}) copy-start(bf16[16,256,256]{2,1,0:T(8,128)(2,1)S(1)} %all-to-all-done.1) | copy-start | bytes 6291460
  120.7 0.9 copy-start.8
  162.9 7.4 %copy-start.10 = (bf16[1024,256]{1,0:T(8,128)(2,1)S(1)}, bf16[1024,256]{1,0:T(8,128)(2,1)}, u32[]{:S(2)}) copy-start(bf16[1024,256]{1,0:T(8,128)(2,1)} %get-tuple-element.22) | copy-start | bytes 1572868
  162.9 45.3 %all-to-all-start.3 = ((bf16[16,256,256]{2,1,0:T(8,128)(2,1)}), bf16[16,256,256]{2,1,0:T(8,128)(2,1)S(1)}, u32[]{:S(2)}, u32[]{:S(2)}) async-start(bf16[16,256,256]{2,1,0:T(8,128)(2,1)} %bitcast.51), calls=%async_computation.3 | async-start | bytes 4194304 | tf_op jit(solution)/shard_map/all_to_all | solution.py:204
  170.3 36.9 %collective-permute-start.1 = (bf16[1024,256]{1,0:T(8,128)(2,1)S(1)}, bf16[1024,256]{1,0:T(8,128)(2,1)S(1)}, u32[]{:S(2)}, u32[]{:S(2)}) collective-permute-start(bf16[1024,256]{1,0:T(8,128)(2,1)S(1)} %copy-done.10), channel_id=1, source_target_pairs={{16,0},{32,16},{48,32},{64,48},{80,64},{96,80},{112,96},{17,1},{33... | collective-permute-start | bytes 1572872 | tf_op jit(solution)/shard_map/ppermute | solution.py:21
  208.2 36.4 %all-to-all-start.2 = ((bf16[16,256,256]{2,1,0:T(8,128)(2,1)}), bf16[16,256,256]{2,1,0:T(8,128)(2,1)}, u32[]{:S(2)}, u32[]{:S(2)}) async-start(bf16[16,256,256]{2,1,0:T(8,128)(2,1)} %bitcast.52), calls=%async_computation.2 | async-start | bytes 4194304 | tf_op jit(solution)/shard_map/all_to_all | solution.py:204
  215.5 3.2 %copy-start.3 = (f32[4096,128]{1,0:T(8,128)S(1)}, f32[4096,128]{1,0:T(8,128)}, u32[]{:S(2)}) copy-start(f32[4096,128]{1,0:T(8,128)} %get-tuple-element.19) | copy-start | bytes 6291460
  215.5 3.8 %copy-start.4 = (f32[4096,128]{1,0:T(8,128)S(1)}, f32[4096,128]{1,0:T(8,128)}, u32[]{:S(2)}) copy-start(f32[4096,128]{1,0:T(8,128)} %get-tuple-element.20) | copy-start | bytes 6291460
  215.5 3.9 %copy-start.5 = (f32[1024,128]{1,0:T(8,128)S(1)}, f32[1024,128]{1,0:T(8,128)}, u32[]{:S(2)}) copy-start(f32[1024,128]{1,0:T(8,128)} %slice.54) | copy-start | bytes 1572868
  215.5 4.0 %copy-start.7 = (f32[1024,128]{1,0:T(8,128)S(1)}, f32[1024,128]{1,0:T(8,128)}, u32[]{:S(2)}) copy-start(f32[1024,128]{1,0:T(8,128)} %get-tuple-element.36) | copy-start | bytes 1572868
  244.6 33.5 %all-to-all-start.4 = ((bf16[16,256,256]{2,1,0:T(8,128)(2,1)}), bf16[16,256,256]{2,1,0:T(8,128)(2,1)}, u32[]{:S(2)}, u32[]{:S(2)}) async-start(bf16[16,256,256]{2,1,0:T(8,128)(2,1)} %bitcast.48), calls=%async_computation.4 | async-start | bytes 4194304 | tf_op jit(solution)/shard_map/all_to_all | solution.py:204
  279.9 2.5 copy-start.1

commit v3 on v2

--- a/solution.py
+++ b/solution.py
@@ -45,7 +45,9 @@
     bias_ref = refs[pos]
     pos += 1
     if early:
-        kx_ref, vx_ref = refs[pos : pos + 2]
+        kx_ref, vx_ref, dkx_ref, dvx_ref = refs[pos : pos + 4]
+        dk_out_ref, dv_out_ref = dk_ref, dv_ref
+        dk_ref, dv_ref = dkx_ref, dvx_ref
     step = pl.program_id(0)
     block = step + block_offset
     rows = q_refs[0].shape[0]
@@ -113,13 +115,15 @@
         def _():
             halo_ref[:, :HD] = dk_ref[:WIN, :].astype(jnp.bfloat16)
             halo_ref[:, HD:] = dv_ref[:WIN, :].astype(jnp.bfloat16)
+            dk_out_ref[...] = dk_ref[WIN:, :]
+            dv_out_ref[...] = dv_ref[WIN:, :]
 
 
 def attend(sources, first_part, tail, first_query, blocks, carried_od):
     heads = len(sources)
     query_count = first_part.shape[0]
     acc_base = 0 if tail is not None else WIN
-    acc_rows = 2 * WIN if tail is not None else query_count
+    acc_rows = WIN if tail is not None else query_count
     rows = BLK
     span = WIN + rows
     block_offset, block_count = blocks
@@ -159,6 +163,7 @@
     scratch = [pltpu.VMEM((rows, span), jnp.float32)]
     if early:
         scratch += [pltpu.VMEM((2 * WIN, HD), jnp.bfloat16)] * 2
+        scratch += [pltpu.VMEM((2 * WIN, HD), jnp.float32)] * 2
     grid_spec = pltpu.PrefetchScalarGridSpec(
         num_scalar_prefetch=1,
         grid=(block_count,),
@@ -239,12 +244,12 @@
     lead_pad = ((0, group_rows - WIN), (0, 0))
     tail_pad = ((group_rows - WIN, 0), (0, 0))
     key_grad = (
-        key_late + key_last + jnp.pad(key_early[WIN:], lead_pad) + jnp.pad(back[:, :HD], tail_pad)
+        key_late + key_last + jnp.pad(key_early, lead_pad) + jnp.pad(back[:, :HD], tail_pad)
     ).astype(jnp.bfloat16)
     value_grad = (
         value_late
         + value_last
-        + jnp.pad(value_early[WIN:], lead_pad)
+        + jnp.pad(value_early, lead_pad)
         + jnp.pad(back[:, HD:], tail_pad)
     ).astype(jnp.bfloat16)
     grads_back = exchange_out(jnp.concatenate([key_grad, value_grad], axis=1))

time: 284 us -> 283 us (level)
  local copies, waits for them, and re-layouts: 24.8 us -> 20.1 us
  waiting for transfers between devices: 142 us -> 146 us
    slice x2 -> x0, local copies, waits for them, and re-layouts: 3.75 us -> none  [the longest x1 1.89 us: body(): key_early[WIN:]]
    ppermute x2, waiting for transfers between devices: 36.5 us -> 40.2 us  [shifted(): return lax.ppermute(block, axis, route)]
    unnamed x29 -> x27, local copies, waits for them, and re-layouts: 9.91 us -> 9.71 us
  transfers between devices with their start and end apart: 7 -> 7, of which waited for: 5 -> 5; matrix products, arithmetic and copies ran while one was open for 7% -> 5% of each run, Pallas kernels for 9% -> 9%
where the time goes in v3:
time: 283 us; the launch traced here: 281 us
  waiting for transfers between devices  146 us (52%)
  Pallas kernels  66 us (23%)
  starting transfers between devices  38.8 us (14%)
  local copies, waits for them, and re-layouts  20.1 us (7%)
  other arithmetic  9.15 us (3%)
    pallas_call x3, Pallas kernels, attend(): pl.pallas_call(kernel, grid_spec=grid_spec, out_shape=[jax.ShapeDtypeStru...  66 us
    all_to_all x2, waiting for transfers between devices, exchange_in(): lax.all_to_all(stacked, 'head', split_axis=0, concat_axis=0, tiled=True)  59.2 us
    all_to_all x3, waiting for transfers between devices, exchange_out(): lax.all_to_all(split, 'head', split_axis=0, concat_axis=0, tiled=True)  46.8 us
    ppermute x2, waiting for transfers between devices, shifted(): return lax.ppermute(block, axis, route)  40.2 us
    all_to_all x3, starting transfers between devices, exchange_out(): lax.all_to_all(split, 'head', split_axis=0, concat_axis=0, tiled=True)  18.9 us
    all_to_all x2, starting transfers between devices, exchange_in(): lax.all_to_all(stacked, 'head', split_axis=0, concat_axis=0, tiled=True)  11.9 us
    unnamed x27, local copies, waits for them, and re-layouts  9.71 us
    ppermute x2, starting transfers between devices, shifted(): return lax.ppermute(block, axis, route)  8.05 us
  transfers between devices with their start and end apart: 7, of which 5 were waited for; matrix products, arithmetic and copies ran while one was open for 5% of the time, Pallas kernels for 9%

profile of v3, /device:TPU:121, one launch (start us, length us, event | category | flops | bytes accessed | tf_op | source)
XLA Modules:
  0.0 281.1 jit_solution(3078423309871409986)
XLA Ops:
  0.6 2.3 copy.30
  3.6 1.3 copy-done.5
  4.9 0.6 copy.31
  6.3 0.9 copy-done.7
  7.7 2.3 maximum_bitcast_fusion
  10.0 5.9 %all-to-all-start = ((bf16[16,256,512]{2,1,0:T(8,128)(2,1)}), bf16[16,256,512]{2,1,0:T(8,128)(2,1)}, u32[]{:S(2)}, u32[]{:S(2)}) async-start(bf16[16,256,512]{2,1,0:T(8,128)(2,1)} %maximum_bitcast_fusion), calls=%async_computation | async-start | bytes 8388608 | tf_op jit(solution)/shard_map/all_to_all | solution.py:202
  16.5 1.6 maximum_bitcast_fusion.1
  18.1 59.2 %all-to-all-done = bf16[16,256,512]{2,1,0:T(8,128)(2,1)} async-done(((bf16[16,256,512]{2,1,0:T(8,128)(2,1)}), bf16[16,256,512]{2,1,0:T(8,128)(2,1)}, u32[]{:S(2)}, u32[]{:S(2)}) %all-to-all-start) | async-done | bytes 4194336 | tf_op jit(solution)/shard_map/all_to_all | solution.py:202
  77.3 5.9 %all-to-all-start.1 = ((bf16[16,256,256]{2,1,0:T(8,128)(2,1)}), bf16[16,256,256]{2,1,0:T(8,128)(2,1)S(1)}, u32[]{:S(2)}, u32[]{:S(2)}) async-start(bf16[16,256,256]{2,1,0:T(8,128)(2,1)} %maximum_bitcast_fusion.1), calls=%async_computation.1 | async-start | bytes 4194304 | tf_op jit(solution)/shard_map/all_to_all | solution.py:202
  83.2 1.1 slice.56
  84.3 4.5 %collective-permute-start = (bf16[1024,256]{1,0:T(8,128)(2,1)S(1)}, bf16[1024,256]{1,0:T(8,128)(2,1)S(1)}, u32[]{:S(2)}, u32[]{:S(2)}) collective-permute-start(bf16[1024,256]{1,0:T(8,128)(2,1)S(1)} %slice.56), channel_id=1, source_target_pairs={{0,16},{16,32},{32,48},{48,64},{64,80},{80,96},{96,112},{1,17},{17... | collective-permute-start | bytes 1572872 | tf_op jit(solution)/shard_map/ppermute | solution.py:21
  88.9 24.9 %shard_map.75 = (bf16[4096,256]{1,0:T(8,128)(2,1)}, f32[4096,128]{1,0:T(8,128)}, f32[4096,128]{1,0:T(8,128)}) custom-call(s32[1]{0:T(128)} %bitcast.first_ref, bf16[4096,512]{1,0:T(8,128)(2,1)} %bitcast.2.refs_0_.refs_1_.refs_2_.refs_3_.refs_6_.refs_7_, bf16[4096,512]{1,0:T(8,128)(2,1)} %bitcast.2.refs_0_.refs_1_.refs_2_.refs_3_.refs_6_.refs_7_, ...), custom_call_target="tpu_custom_call" | custom-call | tf_op jit(solution)/shard_map/pallas_call | solution.py:184
  113.8 6.8 %collective-permute-done.refs_4_.refs_5_ = bf16[1024,256]{1,0:T(8,128)(2,1)S(1)} collective-permute-done((bf16[1024,256]{1,0:T(8,128)(2,1)S(1)}, bf16[1024,256]{1,0:T(8,128)(2,1)S(1)}, u32[]{:S(2)}, u32[]{:S(2)}) %collective-permute-start) | collective-permute-done | bytes 524320 | tf_op jit(solution)/shard_map/ppermute | solution.py:21
  120.7 0.8 copy-done.6
  121.5 16.2 %shard_map.76 = (bf16[4096,256]{1,0:T(8,128)(2,1)}, bf16[4096,256]{1,0:T(8,128)(2,1)}, f32[1024,128]{1,0:T(8,128)}, f32[1024,128]{1,0:T(8,128)}, bf16[1024,256]{1,0:T(8,128)(2,1)}) custom-call(s32[1]{0:T(128)} %bitcast.first_ref, bf16[4096,512]{1,0:T(8,128)(2,1)} %bitcast.2.refs_0_.refs_1_.refs_2_.refs_3_.refs_6_.refs_7_, ...), custom_call_target="tpu_custom_call", output_to_operand_aliasing={{0}: (9, {})} | custom-call | tf_op jit(solution)/shard_map/pallas_call | solution.py:184
  137.7 24.9 %shard_map.77 = (bf16[4096,256]{1,0:T(8,128)(2,1)}, f32[4096,128]{1,0:T(8,128)}, f32[4096,128]{1,0:T(8,128)}) custom-call(s32[1]{0:T(128)} %bitcast.first_ref, bf16[4096,256]{1,0:T(8,128)(2,1)} %bitcast.45, bf16[4096,256]{1,0:T(8,128)(2,1)} %bitcast.46, ...), custom_call_target="tpu_custom_call", output_to_operand_aliasing={{0}: (5, {})} | custom-call | tf_op jit(solution)/shard_map/pallas_call | solution.py:184
  162.5 7.4 %all-to-all-start.3 = ((bf16[16,256,256]{2,1,0:T(8,128)(2,1)}), bf16[16,256,256]{2,1,0:T(8,128)(2,1)S(1)}, u32[]{:S(2)}, u32[]{:S(2)}) async-start(bf16[16,256,256]{2,1,0:T(8,128)(2,1)} %bitcast.51), calls=%async_computation.3 | async-start | bytes 4194304 | tf_op jit(solution)/shard_map/all_to_all | solution.py:209
  169.9 3.5 %collective-permute-start.1 = (bf16[1024,256]{1,0:T(8,128)(2,1)S(1)}, bf16[1024,256]{1,0:T(8,128)(2,1)S(1)}, u32[]{:S(2)}, u32[]{:S(2)}) collective-permute-start(bf16[1024,256]{1,0:T(8,128)(2,1)S(1)} %copy-done.9), channel_id=1, source_target_pairs={{16,0},{32,16},{48,32},{64,48},{80,64},{96,80},{112,96},{17,1},{33... | collective-permute-start | bytes 1572872 | tf_op jit(solution)/shard_map/ppermute | solution.py:21
  173.4 33.4 %collective-permute-done.1 = bf16[1024,256]{1,0:T(8,128)(2,1)S(1)} collective-permute-done((bf16[1024,256]{1,0:T(8,128)(2,1)S(1)}, bf16[1024,256]{1,0:T(8,128)(2,1)S(1)}, u32[]{:S(2)}, u32[]{:S(2)}) %collective-permute-start.1) | collective-permute-done | bytes 524320 | tf_op jit(solution)/shard_map/ppermute | solution.py:21
  206.9 7.2 %all-to-all-start.2 = ((bf16[16,256,256]{2,1,0:T(8,128)(2,1)}), bf16[16,256,256]{2,1,0:T(8,128)(2,1)}, u32[]{:S(2)}, u32[]{:S(2)}) async-start(bf16[16,256,256]{2,1,0:T(8,128)(2,1)} %bitcast.52), calls=%async_computation.2 | async-start | bytes 4194304 | tf_op jit(solution)/shard_map/all_to_all | solution.py:209
  214.1 2.8 add_convert_fusion
  217.1 0.6 copy-done.4
  218.1 1.6 pad_maximum_fusion
  219.7 23.6 %all-to-all-done.2 = bf16[16,256,256]{2,1,0:T(8,128)(2,1)} async-done(((bf16[16,256,256]{2,1,0:T(8,128)(2,1)}), bf16[16,256,256]{2,1,0:T(8,128)(2,1)}, u32[]{:S(2)}, u32[]{:S(2)}) %all-to-all-start.2) | async-done | bytes 2097184 | tf_op jit(solution)/shard_map/all_to_all | solution.py:209
  243.3 4.3 %all-to-all-start.4 = ((bf16[16,256,256]{2,1,0:T(8,128)(2,1)}), bf16[16,256,256]{2,1,0:T(8,128)(2,1)}, u32[]{:S(2)}, u32[]{:S(2)}) async-start(bf16[16,256,256]{2,1,0:T(8,128)(2,1)} %bitcast.48), calls=%async_computation.4 | async-start | bytes 4194304 | tf_op jit(solution)/shard_map/all_to_all | solution.py:209
  248.2 1.7 fusion
  250.2 1.6 copy.27
  252.1 1.6 copy.26
  253.6 23.2 %all-to-all-done.4 = bf16[16,256,256]{2,1,0:T(8,128)(2,1)} async-done(((bf16[16,256,256]{2,1,0:T(8,128)(2,1)}), bf16[16,256,256]{2,1,0:T(8,128)(2,1)}, u32[]{:S(2)}, u32[]{:S(2)}) %all-to-all-start.4) | async-done | bytes 2097184 | tf_op jit(solution)/shard_map/all_to_all | solution.py:209
  276.8 1.7 slice_bitcast_fusion
  278.5 1.3 copy.36
  279.8 1.3 copy.37
  (30 shorter events, 4.2 us)
Async XLA Ops:
  0.6 5.6 %copy-start = (bf16[256,2048]{1,0:T(8,128)(2,1)S(1)}, bf16[256,2048]{1,0:T(8,128)(2,1)}, u32[]{:S(2)}) copy-start(bf16[256,2048]{1,0:T(8,128)(2,1)} %param.5) | copy-start | bytes 3145732
  3.3 1.6 copy-start.5
  6.0 1.2 copy-start.7
  10.0 67.3 %all-to-all-start = ((bf16[16,256,512]{2,1,0:T(8,128)(2,1)}), bf16[16,256,512]{2,1,0:T(8,128)(2,1)}, u32[]{:S(2)}, u32[]{:S(2)}) async-start(bf16[16,256,512]{2,1,0:T(8,128)(2,1)} %maximum_bitcast_fusion), calls=%async_computation | async-start | bytes 8388608 | tf_op jit(solution)/shard_map/all_to_all | solution.py:202
  77.3 36.5 %all-to-all-start.1 = ((bf16[16,256,256]{2,1,0:T(8,128)(2,1)}), bf16[16,256,256]{2,1,0:T(8,128)(2,1)S(1)}, u32[]{:S(2)}, u32[]{:S(2)}) async-start(bf16[16,256,256]{2,1,0:T(8,128)(2,1)} %maximum_bitcast_fusion.1), calls=%async_computation.1 | async-start | bytes 4194304 | tf_op jit(solution)/shard_map/all_to_all | solution.py:202
  84.3 36.4 %collective-permute-start = (bf16[1024,256]{1,0:T(8,128)(2,1)S(1)}, bf16[1024,256]{1,0:T(8,128)(2,1)S(1)}, u32[]{:S(2)}, u32[]{:S(2)}) collective-permute-start(bf16[1024,256]{1,0:T(8,128)(2,1)S(1)} %slice.56), channel_id=1, source_target_pairs={{0,16},{16,32},{32,48},{48,64},{64,80},{80,96},{96,112},{1,17},{17... | collective-permute-start | bytes 1572872 | tf_op jit(solution)/shard_map/ppermute | solution.py:21
  113.8 6.9 %copy-start.2 = (bf16[16,256,256]{2,1,0:T(8,128)(2,1)}, bf16[16,256,256]{2,1,0:T(8,128)(2,1)S(1)}, u32[]{:S(2)}) copy-start(bf16[16,256,256]{2,1,0:T(8,128)(2,1)S(1)} %all-to-all-done.1) | copy-start | bytes 6291460
  120.7 0.8 copy-start.6
  162.5 7.4 %copy-start.9 = (bf16[1024,256]{1,0:T(8,128)(2,1)S(1)}, bf16[1024,256]{1,0:T(8,128)(2,1)}, u32[]{:S(2)}) copy-start(bf16[1024,256]{1,0:T(8,128)(2,1)} %get-tuple-element.22) | copy-start | bytes 1572868
  162.5 44.3 %all-to-all-start.3 = ((bf16[16,256,256]{2,1,0:T(8,128)(2,1)}), bf16[16,256,256]{2,1,0:T(8,128)(2,1)S(1)}, u32[]{:S(2)}, u32[]{:S(2)}) async-start(bf16[16,256,256]{2,1,0:T(8,128)(2,1)} %bitcast.51), calls=%async_computation.3 | async-start | bytes 4194304 | tf_op jit(solution)/shard_map/all_to_all | solution.py:209
  169.9 36.9 %collective-permute-start.1 = (bf16[1024,256]{1,0:T(8,128)(2,1)S(1)}, bf16[1024,256]{1,0:T(8,128)(2,1)S(1)}, u32[]{:S(2)}, u32[]{:S(2)}) collective-permute-start(bf16[1024,256]{1,0:T(8,128)(2,1)S(1)} %copy-done.9), channel_id=1, source_target_pairs={{16,0},{32,16},{48,32},{64,48},{80,64},{96,80},{112,96},{17,1},{33... | collective-permute-start | bytes 1572872 | tf_op jit(solution)/shard_map/ppermute | solution.py:21
  206.9 36.4 %all-to-all-start.2 = ((bf16[16,256,256]{2,1,0:T(8,128)(2,1)}), bf16[16,256,256]{2,1,0:T(8,128)(2,1)}, u32[]{:S(2)}, u32[]{:S(2)}) async-start(bf16[16,256,256]{2,1,0:T(8,128)(2,1)} %bitcast.52), calls=%async_computation.2 | async-start | bytes 4194304 | tf_op jit(solution)/shard_map/all_to_all | solution.py:209
  214.1 3.0 %copy-start.3 = (f32[4096,128]{1,0:T(8,128)S(1)}, f32[4096,128]{1,0:T(8,128)}, u32[]{:S(2)}) copy-start(f32[4096,128]{1,0:T(8,128)} %get-tuple-element.19) | copy-start | bytes 6291460
  214.1 3.6 %copy-start.4 = (f32[4096,128]{1,0:T(8,128)S(1)}, f32[4096,128]{1,0:T(8,128)}, u32[]{:S(2)}) copy-start(f32[4096,128]{1,0:T(8,128)} %get-tuple-element.20) | copy-start | bytes 6291460
  214.1 3.7 %copy-start.8 = (f32[1024,128]{1,0:T(8,128)S(1)}, f32[1024,128]{1,0:T(8,128)}, u32[]{:S(2)}) copy-start(f32[1024,128]{1,0:T(8,128)} %get-tuple-element.21) | copy-start | bytes 1572868
  243.3 33.5 %all-to-all-start.4 = ((bf16[16,256,256]{2,1,0:T(8,128)(2,1)}), bf16[16,256,256]{2,1,0:T(8,128)(2,1)}, u32[]{:S(2)}, u32[]{:S(2)}) async-start(bf16[16,256,256]{2,1,0:T(8,128)(2,1)} %bitcast.48), calls=%async_computation.4 | async-start | bytes 4194304 | tf_op jit(solution)/shard_map/all_to_all | solution.py:209
  278.5 2.5 copy-start.1

commit v4 on v3

--- a/solution.py
+++ b/solution.py
@@ -113,8 +113,8 @@
 
         @pl.when(step == pl.num_programs(0) - 1)
         def _():
-            halo_ref[:, :HD] = dk_ref[:WIN, :].astype(jnp.bfloat16)
-            halo_ref[:, HD:] = dv_ref[:WIN, :].astype(jnp.bfloat16)
+            halo_ref[:, :HD] = dk_ref[:WIN, :]
+            halo_ref[:, HD:] = dv_ref[:WIN, :]
             dk_out_ref[...] = dk_ref[WIN:, :]
             dv_out_ref[...] = dv_ref[WIN:, :]
 
@@ -189,7 +189,7 @@
             jax.ShapeDtypeStruct((acc_rows, HD), jnp.float32),
             jax.ShapeDtypeStruct((acc_rows, HD), jnp.float32),
         ]
-        + ([jax.ShapeDtypeStruct((WIN, 2 * HD), jnp.bfloat16)] if early else []),
+        + ([jax.ShapeDtypeStruct((WIN, 2 * HD), jnp.float32)] if early else []),
         input_output_aliases=aliases,
         compiler_params=pltpu.CompilerParams(
             dimension_semantics=("arbitrary",), vmem_limit_bytes=56 * 1024 * 1024
@@ -232,9 +232,15 @@
     head0 = (first_part, 2, 3)
     head1 = (second_part, 0, 1)
     first_out, key_late, value_late = attend([head0], first_part, None, first_query, late, (None,))
-    first_out, second_out, key_early, value_early, halo_part = attend(
-        [head0, head1], first_part, tail, first_query, early, (first_out, None)
-    )
+    first_out, key_early0, value_early0, halo0 = attend(
+        [head0], first_part, tail, first_query, early, (first_out,)
+    )
+    second_out, key_early1, value_early1, halo1 = attend(
+        [head1], first_part, tail, first_query, early, (None,)
+    )
+    key_early = key_early0 + key_early1
+    value_early = value_early0 + value_early1
+    halo_part = (halo0 + halo1).astype(jnp.bfloat16)
     back = shifted(halo_part, "ctx", -1).astype(jnp.float32)
     second_out, key_last, value_last = attend(
         [head1], first_part, None, first_query, late, (second_out,)

time: 283 us -> 293 us (1.035)
  Pallas kernels: 66 us -> 70.3 us
  other arithmetic: 9.15 us -> 12.5 us
  waiting for transfers between devices: 146 us -> 149 us
    all_to_all x2, waiting for transfers between devices: 59.2 us -> 83.8 us  [exchange_in(): lax.all_to_all(stacked, 'head', split_axis=0, concat_axis=0, tiled=True)]
    ppermute x2, waiting for transfers between devices: 40.2 us -> 18.6 us  [shifted(): return lax.ppermute(block, axis, route)]
    pallas_call x3 -> x4, Pallas kernels: 66 us -> 70.3 us  [attend(): pl.pallas_call(kernel, grid_spec=grid_spec, out_shape=[jax.ShapeDtypeStru...]
    unnamed x27 -> x37, local copies, waits for them, and re-layouts: 9.71 us -> 9.84 us
  transfers between devices with their start and end apart: 7 -> 7, of which waited for: 5 -> 6; matrix products, arithmetic and copies ran while one was open for 5% -> 6% of each run, Pallas kernels for 9% -> 12%
where the time goes in v4:
time: 293 us; the launch traced here: 292 us
  waiting for transfers between devices  149 us (51%)
  Pallas kernels  70.3 us (24%)
  starting transfers between devices  38.2 us (13%)
  local copies, waits for them, and re-layouts  20.9 us (7%)
  other arithmetic  12.5 us (4%)
    all_to_all x2, waiting for transfers between devices, exchange_in(): lax.all_to_all(stacked, 'head', split_axis=0, concat_axis=0, tiled=True)  83.8 us
    pallas_call x4, Pallas kernels, attend(): pl.pallas_call(kernel, grid_spec=grid_spec, out_shape=[jax.ShapeDtypeStru...  70.3 us
    all_to_all x3, waiting for transfers between devices, exchange_out(): lax.all_to_all(split, 'head', split_axis=0, concat_axis=0, tiled=True)  46.9 us
    ppermute x2, waiting for transfers between devices, shifted(): return lax.ppermute(block, axis, route)  18.6 us
    all_to_all x3, starting transfers between devices, exchange_out(): lax.all_to_all(split, 'head', split_axis=0, concat_axis=0, tiled=True)  18.5 us
    all_to_all x2, starting transfers between devices, exchange_in(): lax.all_to_all(stacked, 'head', split_axis=0, concat_axis=0, tiled=True)  11.9 us
    unnamed x37, local copies, waits for them, and re-layouts  9.84 us
    ppermute x2, starting transfers between devices, shifted(): return lax.ppermute(block, axis, route)  7.86 us
  transfers between devices with their start and end apart: 7, of which 6 were waited for; matrix products, arithmetic and copies ran while one was open for 6% of the time, Pallas kernels for 12%

profile of v4, /device:TPU:121, one launch (start us, length us, event | category | flops | bytes accessed | tf_op | source)
XLA Modules:
  0.0 292.1 jit_solution(10250789888893951804)
XLA Ops:
  0.6 2.3 copy.30
  3.6 1.3 copy-done.7
  7.7 2.3 maximum_bitcast_fusion
  10.1 5.9 %all-to-all-start = ((bf16[16,256,512]{2,1,0:T(8,128)(2,1)}), bf16[16,256,512]{2,1,0:T(8,128)(2,1)}, u32[]{:S(2)}, u32[]{:S(2)}) async-start(bf16[16,256,512]{2,1,0:T(8,128)(2,1)} %maximum_bitcast_fusion), calls=%async_computation | async-start | bytes 8388608 | tf_op jit(solution)/shard_map/all_to_all | solution.py:202
  16.5 1.6 maximum_bitcast_fusion.1
  18.1 59.2 %all-to-all-done = bf16[16,256,512]{2,1,0:T(8,128)(2,1)} async-done(((bf16[16,256,512]{2,1,0:T(8,128)(2,1)}), bf16[16,256,512]{2,1,0:T(8,128)(2,1)}, u32[]{:S(2)}, u32[]{:S(2)}) %all-to-all-start) | async-done | bytes 4194336 | tf_op jit(solution)/shard_map/all_to_all | solution.py:202
  77.3 5.9 %all-to-all-start.2 = ((bf16[16,256,256]{2,1,0:T(8,128)(2,1)}), bf16[16,256,256]{2,1,0:T(8,128)(2,1)S(1)}, u32[]{:S(2)}, u32[]{:S(2)}) async-start(bf16[16,256,256]{2,1,0:T(8,128)(2,1)} %maximum_bitcast_fusion.1), calls=%async_computation.2 | async-start | bytes 4194304 | tf_op jit(solution)/shard_map/all_to_all | solution.py:202
  83.3 1.1 slice.54
  84.3 4.4 %collective-permute-start = (bf16[1024,256]{1,0:T(8,128)(2,1)S(1)}, bf16[1024,256]{1,0:T(8,128)(2,1)S(1)}, u32[]{:S(2)}, u32[]{:S(2)}) collective-permute-start(bf16[1024,256]{1,0:T(8,128)(2,1)S(1)} %slice.54), channel_id=1, source_target_pairs={{0,16},{16,32},{32,48},{48,64},{64,80},{80,96},{96,112},{1,17},{17... | collective-permute-start | bytes 1572872 | tf_op jit(solution)/shard_map/ppermute | solution.py:21
  88.7 24.6 %all-to-all-done.2 = bf16[16,256,256]{2,1,0:T(8,128)(2,1)S(1)} async-done(((bf16[16,256,256]{2,1,0:T(8,128)(2,1)}), bf16[16,256,256]{2,1,0:T(8,128)(2,1)S(1)}, u32[]{:S(2)}, u32[]{:S(2)}) %all-to-all-start.2) | async-done | bytes 2097184 | tf_op jit(solution)/shard_map/all_to_all | solution.py:202
  113.3 7.4 %collective-permute-done.refs_2_.refs_3_ = bf16[1024,256]{1,0:T(8,128)(2,1)S(1)} collective-permute-done((bf16[1024,256]{1,0:T(8,128)(2,1)S(1)}, bf16[1024,256]{1,0:T(8,128)(2,1)S(1)}, u32[]{:S(2)}, u32[]{:S(2)}) %collective-permute-start) | collective-permute-done | bytes 524320 | tf_op jit(solution)/shard_map/ppermute | solution.py:21
  121.5 10.2 %shard_map.77 = (bf16[4096,256]{1,0:T(8,128)(2,1)}, f32[1024,128]{1,0:T(8,128)}, f32[1024,128]{1,0:T(8,128)}, f32[1024,256]{1,0:T(8,128)}) custom-call(s32[1]{0:T(128)} %bitcast.first_ref, bf16[4096,256]{1,0:T(8,128)(2,1)} %bitcast.43, bf16[4096,256]{1,0:T(8,128)(2,1)} %bitcast.44, bf16[1024,256]{1,0:T(8,128)(2,1)} %copy-done.3, ...), custom_call_target="tpu_custom_call" | custom-call | tf_op jit(solution)/shard_map/pallas_call | solution.py:184
  131.6 24.9 %shard_map.78 = (bf16[4096,256]{1,0:T(8,128)(2,1)}, f32[4096,128]{1,0:T(8,128)}, f32[4096,128]{1,0:T(8,128)}) custom-call(s32[1]{0:T(128)} %bitcast.first_ref, bf16[4096,256]{1,0:T(8,128)(2,1)} %bitcast.45, bf16[4096,256]{1,0:T(8,128)(2,1)} %bitcast.46, ...), custom_call_target="tpu_custom_call", output_to_operand_aliasing={{0}: (5, {})} | custom-call | tf_op jit(solution)/shard_map/pallas_call | solution.py:184
  156.6 7.2 %all-to-all-start.3 = ((bf16[16,256,256]{2,1,0:T(8,128)(2,1)}), bf16[16,256,256]{2,1,0:T(8,128)(2,1)S(1)}, u32[]{:S(2)}, u32[]{:S(2)}) async-start(bf16[16,256,256]{2,1,0:T(8,128)(2,1)} %bitcast.51), calls=%async_computation.3 | async-start | bytes 4194304 | tf_op jit(solution)/shard_map/all_to_all | solution.py:209
  163.8 24.9 %shard_map.75 = (bf16[4096,256]{1,0:T(8,128)(2,1)}, f32[4096,128]{1,0:T(8,128)}, f32[4096,128]{1,0:T(8,128)}) custom-call(s32[1]{0:T(128)} %bitcast.first_ref, bf16[4096,512]{1,0:T(8,128)(2,1)} %bitcast.2.refs_0_.refs_1_.refs_2_.refs_3_.refs_4_.refs_5_, bf16[4096,512]{1,0:T(8,128)(2,1)} %bitcast.2.refs_0_.refs_1_.refs_2_.refs_3_.refs_4_.refs_5_, ...), custom_call_target="tpu_custom_call" | custom-call | tf_op jit(solution)/shard_map/pallas_call | solution.py:184
  188.7 10.3 %shard_map.76 = (bf16[4096,256]{1,0:T(8,128)(2,1)}, f32[1024,128]{1,0:T(8,128)}, f32[1024,128]{1,0:T(8,128)}, f32[1024,256]{1,0:T(8,128)}) custom-call(s32[1]{0:T(128)} %bitcast.first_ref, bf16[4096,512]{1,0:T(8,128)(2,1)} %bitcast.2.refs_0_.refs_1_.refs_2_.refs_3_.refs_4_.refs_5_, ...), custom_call_target="tpu_custom_call", output_to_operand_aliasing={{0}: (7, {})} | custom-call | tf_op jit(solution)/shard_map/pallas_call | solution.py:184
  199.0 1.5 add_convert_fusion.2
  200.5 3.5 %collective-permute-start.1 = (bf16[1024,256]{1,0:T(8,128)(2,1)S(1)}, bf16[1024,256]{1,0:T(8,128)(2,1)S(1)}, u32[]{:S(2)}, u32[]{:S(2)}) collective-permute-start(bf16[1024,256]{1,0:T(8,128)(2,1)S(1)} %add_convert_fusion.2), channel_id=1, source_target_pairs={{16,0},{32,16},{48,32},{64,48},{80,64},{96,80},{112,96},{17,1},{33... | collective-permute-start | bytes 1572872 | tf_op jit(solution)/shard_map/ppermute | solution.py:21
  205.7 11.2 %collective-permute-done.1 = bf16[1024,256]{1,0:T(8,128)(2,1)S(1)} collective-permute-done((bf16[1024,256]{1,0:T(8,128)(2,1)S(1)}, bf16[1024,256]{1,0:T(8,128)(2,1)S(1)}, u32[]{:S(2)}, u32[]{:S(2)}) %collective-permute-start.1) | collective-permute-done | bytes 524320 | tf_op jit(solution)/shard_map/ppermute | solution.py:21
  217.0 1.0 fusion.4
  218.0 6.6 %all-to-all-start.1 = ((bf16[16,256,256]{2,1,0:T(8,128)(2,1)}), bf16[16,256,256]{2,1,0:T(8,128)(2,1)}, u32[]{:S(2)}, u32[]{:S(2)}) async-start(bf16[16,256,256]{2,1,0:T(8,128)(2,1)} %bitcast.52), calls=%async_computation.1 | async-start | bytes 4194304 | tf_op jit(solution)/shard_map/all_to_all | solution.py:209
  224.6 2.9 %add_convert_fusion = bf16[4096,128]{1,0:T(8,128)(2,1)S(1)} fusion(f32[1024,128]{1,0:T(8,128)} %get-tuple-element.43, f32[1024,128]{1,0:T(8,128)} %add.41, f32[4096,128]{1,0:T(8,128)} %get-tuple-element.28, f32[4096,128]{1,0:T(8,128)} %get-tuple-element.29), kind=kLoop, calls=%fused_computation.5 | loop fusion | flops 2097152 | bytes 6291456 | tf_op jit(solution)/shard_map/convert_element_type | solution.py:260
  228.9 1.6 pad_maximum_fusion
  230.5 23.4 %all-to-all-done.1 = bf16[16,256,256]{2,1,0:T(8,128)(2,1)} async-done(((bf16[16,256,256]{2,1,0:T(8,128)(2,1)}), bf16[16,256,256]{2,1,0:T(8,128)(2,1)}, u32[]{:S(2)}, u32[]{:S(2)}) %all-to-all-start.1) | async-done | bytes 2097184 | tf_op jit(solution)/shard_map/all_to_all | solution.py:209
  253.9 4.7 %all-to-all-start.4 = ((bf16[16,256,256]{2,1,0:T(8,128)(2,1)}), bf16[16,256,256]{2,1,0:T(8,128)(2,1)}, u32[]{:S(2)}, u32[]{:S(2)}) async-start(bf16[16,256,256]{2,1,0:T(8,128)(2,1)} %bitcast.48), calls=%async_computation.4 | async-start | bytes 4194304 | tf_op jit(solution)/shard_map/all_to_all | solution.py:209
  258.9 1.7 fusion
  260.9 1.6 copy.27
  262.8 1.6 copy.26
  264.4 23.5 %all-to-all-done.4 = bf16[16,256,256]{2,1,0:T(8,128)(2,1)} async-done(((bf16[16,256,256]{2,1,0:T(8,128)(2,1)}), bf16[16,256,256]{2,1,0:T(8,128)(2,1)}, u32[]{:S(2)}, u32[]{:S(2)}) %all-to-all-start.4) | async-done | bytes 2097184 | tf_op jit(solution)/shard_map/all_to_all | solution.py:209
  287.9 1.7 slice_bitcast_fusion
  289.5 1.3 copy.36
  290.8 1.3 copy.37
  (44 shorter events, 8.7 us)
Async XLA Ops:
  0.6 5.6 %copy-start = (bf16[256,2048]{1,0:T(8,128)(2,1)S(1)}, bf16[256,2048]{1,0:T(8,128)(2,1)}, u32[]{:S(2)}) copy-start(bf16[256,2048]{1,0:T(8,128)(2,1)} %param.5) | copy-start | bytes 3145732
  3.3 1.6 copy-start.7
  6.0 1.2 copy-start.10
  10.1 67.3 %all-to-all-start = ((bf16[16,256,512]{2,1,0:T(8,128)(2,1)}), bf16[16,256,512]{2,1,0:T(8,128)(2,1)}, u32[]{:S(2)}, u32[]{:S(2)}) async-start(bf16[16,256,512]{2,1,0:T(8,128)(2,1)} %maximum_bitcast_fusion), calls=%async_computation | async-start | bytes 8388608 | tf_op jit(solution)/shard_map/all_to_all | solution.py:202
  77.3 36.0 %all-to-all-start.2 = ((bf16[16,256,256]{2,1,0:T(8,128)(2,1)}), bf16[16,256,256]{2,1,0:T(8,128)(2,1)S(1)}, u32[]{:S(2)}, u32[]{:S(2)}) async-start(bf16[16,256,256]{2,1,0:T(8,128)(2,1)} %maximum_bitcast_fusion.1), calls=%async_computation.2 | async-start | bytes 4194304 | tf_op jit(solution)/shard_map/all_to_all | solution.py:202
  84.3 36.4 %collective-permute-start = (bf16[1024,256]{1,0:T(8,128)(2,1)S(1)}, bf16[1024,256]{1,0:T(8,128)(2,1)S(1)}, u32[]{:S(2)}, u32[]{:S(2)}) collective-permute-start(bf16[1024,256]{1,0:T(8,128)(2,1)S(1)} %slice.54), channel_id=1, source_target_pairs={{0,16},{16,32},{32,48},{48,64},{64,80},{80,96},{96,112},{1,17},{17... | collective-permute-start | bytes 1572872 | tf_op jit(solution)/shard_map/ppermute | solution.py:21
  113.3 7.4 %copy-start.2 = (bf16[16,256,256]{2,1,0:T(8,128)(2,1)}, bf16[16,256,256]{2,1,0:T(8,128)(2,1)S(1)}, u32[]{:S(2)}) copy-start(bf16[16,256,256]{2,1,0:T(8,128)(2,1)S(1)} %all-to-all-done.2) | copy-start | bytes 6291460
  120.7 0.8 copy-start.3
  156.6 61.5 %all-to-all-start.3 = ((bf16[16,256,256]{2,1,0:T(8,128)(2,1)}), bf16[16,256,256]{2,1,0:T(8,128)(2,1)S(1)}, u32[]{:S(2)}, u32[]{:S(2)}) async-start(bf16[16,256,256]{2,1,0:T(8,128)(2,1)} %bitcast.51), calls=%async_computation.3 | async-start | bytes 4194304 | tf_op jit(solution)/shard_map/all_to_all | solution.py:209
  188.7 10.3 %copy-start.9 = (f32[1024,256]{1,0:T(8,128)S(1)}, f32[1024,256]{1,0:T(8,128)}, u32[]{:S(2)}) copy-start(f32[1024,256]{1,0:T(8,128)} %get-tuple-element.27) | copy-start | bytes 3145732
  199.0 5.0 %copy-start.12 = (f32[1024,128]{1,0:T(8,128)S(1)}, f32[1024,128]{1,0:T(8,128)}, u32[]{:S(2)}) copy-start(f32[1024,128]{1,0:T(8,128)} %get-tuple-element.31) | copy-start | bytes 1572868
  199.0 5.0 %copy-start.14 = (f32[1024,128]{1,0:T(8,128)S(1)}, f32[1024,128]{1,0:T(8,128)}, u32[]{:S(2)}) copy-start(f32[1024,128]{1,0:T(8,128)} %get-tuple-element.30) | copy-start | bytes 1572868
  199.0 5.9 %copy-start.11 = (f32[1024,128]{1,0:T(8,128)S(1)}, f32[1024,128]{1,0:T(8,128)}, u32[]{:S(2)}) copy-start(f32[1024,128]{1,0:T(8,128)} %get-tuple-element.25) | copy-start | bytes 1572868
  199.0 5.9 %copy-start.13 = (f32[1024,128]{1,0:T(8,128)S(1)}, f32[1024,128]{1,0:T(8,128)}, u32[]{:S(2)}) copy-start(f32[1024,128]{1,0:T(8,128)} %get-tuple-element.24) | copy-start | bytes 1572868
  200.5 16.5 %collective-permute-start.1 = (bf16[1024,256]{1,0:T(8,128)(2,1)S(1)}, bf16[1024,256]{1,0:T(8,128)(2,1)S(1)}, u32[]{:S(2)}, u32[]{:S(2)}) collective-permute-start(bf16[1024,256]{1,0:T(8,128)(2,1)S(1)} %add_convert_fusion.2), channel_id=1, source_target_pairs={{16,0},{32,16},{48,32},{64,48},{80,64},{96,80},{112,96},{17,1},{33... | collective-permute-start | bytes 1572872 | tf_op jit(solution)/shard_map/ppermute | solution.py:21
  218.0 35.9 %all-to-all-start.1 = ((bf16[16,256,256]{2,1,0:T(8,128)(2,1)}), bf16[16,256,256]{2,1,0:T(8,128)(2,1)}, u32[]{:S(2)}, u32[]{:S(2)}) async-start(bf16[16,256,256]{2,1,0:T(8,128)(2,1)} %bitcast.52), calls=%async_computation.1 | async-start | bytes 4194304 | tf_op jit(solution)/shard_map/all_to_all | solution.py:209
  224.6 3.2 %copy-start.4 = (f32[4096,128]{1,0:T(8,128)S(1)}, f32[4096,128]{1,0:T(8,128)}, u32[]{:S(2)}) copy-start(f32[4096,128]{1,0:T(8,128)} %get-tuple-element.23) | copy-start | bytes 6291460
  224.6 3.8 %copy-start.5 = (f32[4096,128]{1,0:T(8,128)S(1)}, f32[4096,128]{1,0:T(8,128)}, u32[]{:S(2)}) copy-start(f32[4096,128]{1,0:T(8,128)} %get-tuple-element.22) | copy-start | bytes 6291460
  224.6 3.9 %copy-start.6 = (f32[1024,128]{1,0:T(8,128)S(1)}, f32[1024,128]{1,0:T(8,128)}, u32[]{:S(2)}) copy-start(f32[1024,128]{1,0:T(8,128)} %add.36) | copy-start | bytes 1572868
  224.6 4.0 %copy-start.8 = (f32[1024,128]{1,0:T(8,128)S(1)}, f32[1024,128]{1,0:T(8,128)}, u32[]{:S(2)}) copy-start(f32[1024,128]{1,0:T(8,128)} %get-tuple-element.42) | copy-start | bytes 1572868
  253.9 34.0 %all-to-all-start.4 = ((bf16[16,256,256]{2,1,0:T(8,128)(2,1)}), bf16[16,256,256]{2,1,0:T(8,128)(2,1)}, u32[]{:S(2)}, u32[]{:S(2)}) async-start(bf16[16,256,256]{2,1,0:T(8,128)(2,1)} %bitcast.48), calls=%async_computation.4 | async-start | bytes 4194304 | tf_op jit(solution)/shard_map/all_to_all | solution.py:209
  289.5 2.5 copy-start.1
